TPU v7x, 512 devices: a whole 4x4x16 slice. The times are simulated.
512 devices in a mesh: dp: 64 (over z, y_lo, core), expert: 8 (over y_hi, x).
Axes of the slice: x: 4, y: 4 (y_hi: 2, y_lo: 2; y = y_hi * 2 + y_lo), z: 16, core: 2. Of those that a mesh axis runs over, the one named last changes fastest.
Arguments:
- inputs: bfloat16 [256, 3072], P('dp', 'expert'), may hold values from -6 to 6
- routes: int32 [256, 2], P('dp'), may hold values from 0 to 7, all different within a row; in each aligned block of 4 rows (0 to 3, 4 to 7, ...) at most 2 rows name the same one
- combine: float32 [256, 2], P('dp'), may hold values from 0.1 to 1
- cotangent: bfloat16 [256, 3072], P('dp', 'expert'), may hold values from -6 to 6
- w_gate: bfloat16 [8, 3072, 8192], P('expert', None, 'dp'), may hold values from -0.109375 to 0.109375
- w_up: bfloat16 [8, 3072, 8192], P('expert', None, 'dp'), may hold values from -0.109375 to 0.109375
- w_down: bfloat16 [8, 8192, 3072], P('expert', 'dp'), may hold values from -0.0625 to 0.0625
Outputs:
- input_grad: bfloat16 [256, 3072], P('dp', 'expert')
- gate_grad: bfloat16 [8, 3072, 8192], P('expert', None, 'dp')
- up_grad: bfloat16 [8, 3072, 8192], P('expert', None, 'dp')
- down_grad: bfloat16 [8, 8192, 3072], P('expert', 'dp')
Inputs may be any that keep to these rules, and one draw needn't show every extreme that they name: `routes`: each token names two different experts. Among the tokens of one index of dp no expert is named more than 2 times, a bound that some block reaches there.
All inputs are finite; a program needn't handle non-finite values.
Results may differ from a plain program's by a relative error of at most 0.0065.
Values may be sent and summed in bfloat16 or wider, within the bound.
No kernel may reach another device: no remote copies, remote signals or barrier semaphores. Data moves between devices by JAX's collectives and lax.ppermute only.
A program may use at most 64 MiB of HBM per device.

v0:
```python
import jax
import jax.numpy as jnp
from jax import lax
from jax.sharding import PartitionSpec as P

MOST = 2


def forward_part(all_inputs, w_gate, w_up):
    gate_pre = jnp.einsum("rld,ldf->rlf", all_inputs, w_gate, preferred_element_type=jnp.float32)
    up_pre = jnp.einsum("rld,ldf->rlf", all_inputs, w_up, preferred_element_type=jnp.float32)
    gate_sig = jax.nn.sigmoid(gate_pre)
    activated = gate_pre * gate_sig
    hidden = (activated * up_pre).astype(jnp.bfloat16)
    return (gate_pre, up_pre, gate_sig, activated, hidden)


def per_device(inputs, routes, combine, cotangent, w_gate, w_up, w_down):
    local_experts = w_gate.shape[0]
    expert_count = local_experts * lax.axis_size("expert")
    slot_count = MOST
    width_part = inputs.shape[1]
    routes_flat = routes.reshape(-1)
    onehot = (routes_flat[:, None] == jnp.arange(expert_count, dtype=jnp.int32)[None, :]).astype(
        jnp.int32
    )
    before = jnp.cumsum(onehot, axis=0) - onehot
    slot_index = jnp.sum(before * onehot, axis=1)
    column = slot_index * expert_count + routes_flat
    placer = column[:, None] == jnp.arange(slot_count * expert_count, dtype=jnp.int32)[None, :]
    placer_half = placer.astype(jnp.bfloat16)
    repeated = jnp.repeat(inputs, 2, axis=0)
    scaled = (
        combine.reshape(-1)[:, None] * jnp.repeat(cotangent, 2, axis=0).astype(jnp.float32)
    ).astype(jnp.bfloat16)
    sent_inputs = jnp.einsum(
        "jc,jd->cd", placer_half, repeated, preferred_element_type=jnp.float32
    ).astype(jnp.bfloat16)
    sent_grads = jnp.einsum(
        "jc,jd->cd", placer_half, scaled, preferred_element_type=jnp.float32
    ).astype(jnp.bfloat16)
    sent_inputs = sent_inputs.reshape(slot_count, expert_count, width_part)
    sent_grads = sent_grads.reshape(slot_count, expert_count, width_part)
    expert_inputs, expert_grads = (
        lax.all_to_all(sent_inputs, "expert", split_axis=1, concat_axis=2, tiled=True),
        lax.all_to_all(sent_grads, "expert", split_axis=1, concat_axis=2, tiled=True),
    )
    all_inputs, all_grads = (
        lax.all_gather(expert_inputs, "dp", axis=0, tiled=True),
        lax.all_gather(expert_grads, "dp", axis=0, tiled=True),
    )
    gate_pre, up_pre, gate_sig, activated, hidden = forward_part(all_inputs, w_gate, w_up)
    hidden_delta = jnp.einsum("rld,lfd->rlf", all_grads, w_down, preferred_element_type=jnp.float32)
    down_grad = jnp.einsum(
        "rlf,rld->lfd", hidden, all_grads, preferred_element_type=jnp.float32
    ).astype(jnp.bfloat16)
    gate_delta = (hidden_delta * up_pre * gate_sig * (1.0 + gate_pre * (1.0 - gate_sig))).astype(
        jnp.bfloat16
    )
    up_delta = (hidden_delta * activated).astype(jnp.bfloat16)
    gate_grad = jnp.einsum(
        "rld,rlf->ldf", all_inputs, gate_delta, preferred_element_type=jnp.float32
    ).astype(jnp.bfloat16)
    up_grad = jnp.einsum(
        "rld,rlf->ldf", all_inputs, up_delta, preferred_element_type=jnp.float32
    ).astype(jnp.bfloat16)
    from_gate = jnp.einsum("rlf,ldf->rld", gate_delta, w_gate, preferred_element_type=jnp.float32)
    from_up = jnp.einsum("rlf,ldf->rld", up_delta, w_up, preferred_element_type=jnp.float32)
    own_rows = lax.psum_scatter(from_gate + from_up, "dp", scatter_dimension=0, tiled=True)
    back_rows = lax.all_to_all(own_rows, "expert", split_axis=2, concat_axis=1, tiled=True)
    back_flat = back_rows.reshape(slot_count * expert_count, width_part)
    assign_grad = jnp.dot(placer.astype(jnp.float32), back_flat, precision=lax.Precision.HIGHEST)
    input_grad = jnp.sum(assign_grad.reshape(inputs.shape[0], 2, width_part), axis=1).astype(
        jnp.bfloat16
    )
    return (input_grad, gate_grad, up_grad, down_grad)


def solution(mesh):
    placed = (
        P("dp", "expert"),
        P("dp", None),
        P("dp", None),
        P("dp", "expert"),
        P("expert", None, "dp"),
        P("expert", None, "dp"),
        P("expert", "dp", None),
    )
    return jax.shard_map(
        per_device,
        mesh=mesh,
        in_specs=placed,
        out_specs=(
            P("dp", "expert"),
            P("expert", None, "dp"),
            P("expert", None, "dp"),
            P("expert", "dp", None),
        ),
        check_vma=False,
    )
```

profile of v0, /device:TPU:1, one launch (start us, length us, event | category | flops | bytes accessed | tf_op | source)
XLA Modules:
  0.0 658.0 jit_solution(9490560236936488608)
XLA Ops:
  7.2 0.8 copy.37
  10.0 7.5 %all-to-all-start.1 = ((bf16[2,8,384]{2,0,1:T(2,128)(2,1)}), bf16[2,8,384]{2,0,1:T(2,128)(2,1)S(1)}, u32[]{:S(2)}, u32[]{:S(2)}) async-start(bf16[2,8,384]{2,0,1:T(2,128)(2,1)} %copy.43), calls=%async_computation.1 | async-start | bytes 24576 | tf_op jit(solution)/shard_map/all_to_all | solution.py:45
  17.5 0.8 copy.40
  19.9 4.1 all-to-all-done.1
  24.0 3.3 all-to-all-start
  27.4 6.4 all-to-all-done
  33.9 76.2 %all_gather.6 = bf16[128,1,3072]{2,1,0:T(2,128)(2,1)S(1)} all-gather(bf16[2,1,3072]{2,1,0:T(2,128)(2,1)S(1)} %copy.42), channel_id=1, replica_groups=mesh['dp'=64,'expert'=8] {'dp'}, dimensions={0}, use_global_device_ids=true | all-gather | bytes 798720 | tf_op jit(solution)/shard_map/all_gather | solution.py:50
  110.1 63.8 %all_gather.7 = bf16[128,1,3072]{2,1,0:T(2,128)(2,1)S(1)} all-gather(bf16[2,1,3072]{2,1,0:T(2,128)(2,1)S(1)} %copy.44), channel_id=1, replica_groups=mesh['dp'=64,'expert'=8] {'dp'}, dimensions={0}, use_global_device_ids=true | all-gather | bytes 798720 | tf_op jit(solution)/shard_map/all_gather | solution.py:49
  176.1 1.5 fusion
  177.9 1.3 dynamic-slice
  179.8 1.3 fusion.2
  181.1 1.3 fusion.3
  182.4 429.8 %all-reduce.3.cloned.1.call-done = f32[128,1,3072]{2,0,1:T(8,128)} async-done(((f32[128,1,3072]{2,0,1:T(8,128)}), f32[128,1,3072]{2,0,1:T(8,128)}) %all-reduce.3.cloned.1.call-update) | async-done | bytes 1572880
  612.2 0.9 constant_dynamic-slice_fusion
  613.1 1.6 copy.45
  615.2 14.8 %reduce = f32[3072,2]{1,0:T(8,128)} reduce(f32[3072,1,2]{2,1,0:T(1,128)S(1)} %bitcast.92, f32[]{:T(128)} %broadcast.50), dimensions={1}, to_apply=%bitcast.79.reduce_sub_computation | reduce | bytes 49156
  630.0 3.0 reshape.131
  633.1 6.2 all-to-all-start.2
  639.2 1.3 fusion.1
  640.5 5.3 all-to-all-done.2
  645.8 0.7 reduce.1
  646.5 2.5 reshape.132
  649.1 1.3 copy.46
  650.4 0.8 convolution_reduce_fusion
  (34 shorter events, 6.7 us)
Async XLA Ops:
  7.2 166.9 %copy-start = (bf16[1,3072,128]{2,1,0:T(8,128)(2,1)S(1)}, bf16[1,3072,128]{2,1,0:T(8,128)(2,1)}, u32[]{:S(2)}) copy-start(bf16[1,3072,128]{2,1,0:T(8,128)(2,1)} %param.11) | copy-start | bytes 2359300
  10.0 14.0 %all-to-all-start.1 = ((bf16[2,8,384]{2,0,1:T(2,128)(2,1)}), bf16[2,8,384]{2,0,1:T(2,128)(2,1)S(1)}, u32[]{:S(2)}, u32[]{:S(2)}) async-start(bf16[2,8,384]{2,0,1:T(2,128)(2,1)} %copy.43), calls=%async_computation.1 | async-start | bytes 24576 | tf_op jit(solution)/shard_map/all_to_all | solution.py:45
  24.0 9.8 %all-to-all-start = ((bf16[2,8,384]{2,0,1:T(2,128)(2,1)}), bf16[2,8,384]{2,0,1:T(2,128)(2,1)S(1)}, u32[]{:S(2)}, u32[]{:S(2)}) async-start(bf16[2,8,384]{2,0,1:T(2,128)(2,1)} %copy.41), calls=%async_computation | async-start | bytes 24576 | tf_op jit(solution)/shard_map/all_to_all | solution.py:46
  27.4 584.8 %all-reduce.3.cloned.1.call-start = ((), (), s32[]{:S(2)}) async-start(), calls=%async_computation.3 | async-start | bytes 3145728
  173.8 1.1 copy-start.1
  174.1 1.2 copy-start.2
  633.1 12.7 %all-to-all-start.2 = ((f32[8,1,768]{2,1,0:T(1,128)}), f32[8,1,768]{2,1,0:T(1,128)S(1)}, u32[]{:S(2)}, u32[]{:S(2)}) async-start(f32[8,1,768]{2,1,0:T(1,128)} %reshape.131), calls=%async_computation.2 | async-start | bytes 49152 | tf_op jit(solution)/shard_map/all_to_all | solution.py:70
Sparse Core Ops, SparseCore 0:
  177.8 434.3 all-reduce.2
where the time goes:
time: 659 us; the launch traced here: 658 us
  waiting for transfers between devices  446 us (68%)
  blocking collectives  140 us (21%)
  starting transfers between devices  17 us (3%)
  local copies, waits for them, and re-layouts  16.5 us (3%)
  other arithmetic  15.8 us (2%)
  between operations  14.8 us (2%)
  matrix products  8.23 us (1%)
    unnamed x2, waiting for transfers between devices  430 us
    all_gather x1, blocking collectives, per_device(): lax.all_gather(expert_grads, 'dp', axis=0, tiled=True)  76.2 us
    all_gather x1, blocking collectives, per_device(): lax.all_gather(expert_inputs, 'dp', axis=0, tiled=True)  63.8 us
    unnamed x1, other arithmetic  14.8 us
  transfers between devices with their start and end apart: 4, of which 4 were waited for; matrix products, arithmetic and copies ran while one was open for 1% of the time, Pallas kernels for 0%

commit v1 on v0

v1 whole, which is shorter than its diff:
```python
import jax
import jax.numpy as jnp
from jax import lax
from jax.sharding import Mesh, PartitionSpec as P

MOST = 2
DP = ("z", "y_lo", "core")
EX = ("y_hi", "x")


def forward_part(rows_in, w_gate, w_up):
    gate_pre = jnp.dot(rows_in, w_gate, preferred_element_type=jnp.float32)
    up_pre = jnp.dot(rows_in, w_up, preferred_element_type=jnp.float32)
    gate_sig = jax.nn.sigmoid(gate_pre)
    activated = gate_pre * gate_sig
    hidden = (activated * up_pre).astype(jnp.bfloat16)
    return (gate_pre, up_pre, gate_sig, activated, hidden)


def gather_dp(block):
    block = lax.all_gather(block, "core", axis=0)
    block = lax.all_gather(block, "y_lo", axis=0)
    block = lax.all_gather(block, "z", axis=0)
    return block.reshape((-1,) + block.shape[3:])


def per_device(inputs, routes, combine, cotangent, w_gate, w_up, w_down):
    tok = inputs.shape[0]
    width_part = inputs.shape[1]
    n_ex = lax.axis_size(EX)
    n_dp = lax.axis_size(DP)
    capacity = n_dp * MOST
    slots_in_block = 2 * tok

    scaled = (
        combine.reshape(-1)[:, None] * jnp.repeat(cotangent, 2, axis=0).astype(jnp.float32)
    ).astype(jnp.bfloat16)
    route_row = jnp.zeros((1, width_part), jnp.bfloat16)
    route_row = route_row.at[0, :slots_in_block].set(routes.reshape(-1).astype(jnp.bfloat16))
    packed = jnp.concatenate([inputs, scaled, route_row], axis=0)
    pad_rows = (-packed.shape[0]) % 16
    packed = jnp.pad(packed, ((0, pad_rows), (0, 0)))
    every = gather_dp(packed)
    all_in = every[:, :tok, :].reshape(n_dp * tok, width_part)
    all_scaled = every[:, tok : 3 * tok, :].reshape(n_dp * slots_in_block, width_part)
    all_routes = every[:, 3 * tok, :slots_in_block].astype(jnp.int32)

    onehot = (all_routes[:, :, None] == jnp.arange(n_ex, dtype=jnp.int32)).astype(jnp.int32)
    before = jnp.cumsum(onehot, axis=1) - onehot
    rank = jnp.sum(before * onehot, axis=2)
    block_id = jnp.arange(n_dp, dtype=jnp.int32)[:, None]
    column = (all_routes * capacity + block_id * MOST + rank).reshape(-1)
    placer = column[:, None] == jnp.arange(n_ex * capacity, dtype=jnp.int32)[None, :]
    placer_tok = jnp.any(placer.reshape(n_dp * tok, 2, n_ex * capacity), axis=1)

    sent_in = jnp.dot(
        placer_tok.astype(jnp.bfloat16).T, all_in, preferred_element_type=jnp.float32
    ).astype(jnp.bfloat16)
    sent_grad = jnp.dot(
        placer.astype(jnp.bfloat16).T, all_scaled, preferred_element_type=jnp.float32
    ).astype(jnp.bfloat16)
    sent = jnp.concatenate([sent_in, sent_grad], axis=1).reshape(n_ex, capacity, 2 * width_part)
    got = lax.all_to_all(sent, EX, 0, 0, tiled=True)
    got = got.reshape(n_ex, capacity, 2, width_part).transpose(2, 1, 0, 3)
    rows_in = got[0].reshape(capacity, n_ex * width_part)
    rows_grad = got[1].reshape(capacity, n_ex * width_part)

    gate_w, up_w, down_w = w_gate[0], w_up[0], w_down[0]
    gate_pre, up_pre, gate_sig, activated, hidden = forward_part(rows_in, gate_w, up_w)
    hidden_delta = jnp.dot(rows_grad, down_w.T, preferred_element_type=jnp.float32)
    down_grad = jnp.dot(hidden.T, rows_grad, preferred_element_type=jnp.float32).astype(
        jnp.bfloat16
    )
    gate_delta = (hidden_delta * up_pre * gate_sig * (1.0 + gate_pre * (1.0 - gate_sig))).astype(
        jnp.bfloat16
    )
    up_delta = (hidden_delta * activated).astype(jnp.bfloat16)
    gate_grad = jnp.dot(rows_in.T, gate_delta, preferred_element_type=jnp.float32).astype(
        jnp.bfloat16
    )
    up_grad = jnp.dot(rows_in.T, up_delta, preferred_element_type=jnp.float32).astype(jnp.bfloat16)
    from_gate = jnp.dot(gate_delta, gate_w.T, preferred_element_type=jnp.float32)
    from_up = jnp.dot(up_delta, up_w.T, preferred_element_type=jnp.float32)
    partial = (from_gate + from_up).reshape(capacity, n_ex, width_part).transpose(1, 0, 2)
    back = lax.all_to_all(partial, EX, 0, 0, tiled=True).reshape(n_ex * capacity, width_part)
    token_part = jnp.dot(
        placer_tok.astype(jnp.float32), back, precision=lax.Precision.HIGHEST
    )
    owned = lax.all_to_all(token_part.reshape(n_dp, tok, width_part), DP, 0, 0, tiled=True)
    input_grad = jnp.sum(owned, axis=0).astype(jnp.bfloat16)
    return (input_grad, gate_grad[None], up_grad[None], down_grad[None])


def solution(mesh):
    n_dp, n_ex = mesh.shape["dp"], mesh.shape["expert"]
    fine = Mesh(mesh.devices.reshape(n_dp // 4, 2, 2, 2, n_ex // 2), DP + EX)
    placed = (
        P(DP, EX),
        P(DP, None),
        P(DP, None),
        P(DP, EX),
        P(EX, None, DP),
        P(EX, None, DP),
        P(EX, DP, None),
    )
    return jax.shard_map(
        per_device,
        mesh=fine,
        in_specs=placed,
        out_specs=(
            P(DP, EX),
            P(EX, None, DP),
            P(EX, None, DP),
            P(EX, DP, None),
        ),
        check_vma=False,
    )
```

time: 659 us -> 143 us (0.22)
  waiting for transfers between devices: 446 us -> 38.7 us
  blocking collectives: 140 us -> 61.3 us
  between operations: 14.8 us -> 0.85 us
  other arithmetic: 15.8 us -> 4.31 us
  local copies, waits for them, and re-layouts: 16.5 us -> 6.06 us
    unnamed x2 -> x0, waiting for transfers between devices: 430 us -> none
    all_gather x2 -> x3, blocking collectives: 140 us -> 39.7 us  [the longest x1 28 us: gather_dp(): block = lax.all_gather(block, 'z', axis=0)]
    all_to_all x3 -> x2, waiting for transfers between devices: 15.8 us -> 38.7 us  [the longest x1 24.2 us: per_device(): lax.all_to_all(token_part.reshape(n_dp, tok, width_part), DP, 0, 0, tiled...]
    all_to_all x0 -> x1, blocking collectives: none -> 21.5 us  [per_device(): got = lax.all_to_all(sent, EX, 0, 0, tiled=True)]
    unnamed x1 -> x0, other arithmetic: 14.8 us -> none
    unnamed x14 -> x7, local copies, waits for them, and re-layouts: 10.6 us -> 1.47 us
    all_to_all x3 -> x2, starting transfers between devices: 17 us -> 21.9 us  [the longest x1 17.6 us: per_device(): lax.all_to_all(token_part.reshape(n_dp, tok, width_part), DP, 0, 0, tiled...]
  transfers between devices with their start and end apart: 4 -> 2, of which waited for: 4 -> 2; matrix products, arithmetic and copies ran while one was open for 1% -> 3% of each run, Pallas kernels for 0% -> 0%
where the time goes in v1:
time: 143 us
  blocking collectives  61.3 us (43%)
  waiting for transfers between devices  38.7 us (27%)
  starting transfers between devices  21.9 us (15%)
  matrix products  9.45 us (7%)
  local copies, waits for them, and re-layouts  6.06 us (4%)
  other arithmetic  4.31 us (3%)
    all_gather x1, blocking collectives, gather_dp(): block = lax.all_gather(block, 'z', axis=0)  28 us
    all_to_all x1, waiting for transfers between devices, per_device(): lax.all_to_all(token_part.reshape(n_dp, tok, width_part), DP, 0, 0, tiled...  24.2 us
    all_to_all x1, blocking collectives, per_device(): got = lax.all_to_all(sent, EX, 0, 0, tiled=True)  21.5 us
    all_to_all x1, starting transfers between devices, per_device(): lax.all_to_all(token_part.reshape(n_dp, tok, width_part), DP, 0, 0, tiled...  17.6 us
    all_to_all x1, waiting for transfers between devices, per_device(): lax.all_to_all(partial, EX, 0, 0, tiled=True)  14.6 us
    all_gather x1, blocking collectives, gather_dp(): block = lax.all_gather(block, 'core', axis=0)  8.37 us
    all_to_all x1, starting transfers between devices, per_device(): lax.all_to_all(partial, EX, 0, 0, tiled=True)  4.29 us
    all_gather x1, blocking collectives, gather_dp(): block = lax.all_gather(block, 'y_lo', axis=0)  3.34 us
  transfers between devices with their start and end apart: 2, of which 2 were waited for; matrix products, arithmetic and copies ran while one was open for 3% of the time, Pallas kernels for 0%

profile of v1, /device:TPU:1, one launch (start us, length us, event | category | flops | bytes accessed | tf_op | source)
XLA Modules:
  0.0 142.5 jit_solution(14898471504535880717)
XLA Ops:
  0.6 0.6 compare_reduce_fusion
  1.3 1.3 broadcast_select_fusion
  2.8 0.7 broadcast_in_dim.8
  3.5 0.8 copy.29
  4.4 0.7 fusion.23
  5.2 8.4 %all-gather = bf16[32,384]{1,0:T(8,128)(2,1)S(1)} all-gather(bf16[16,384]{1,0:T(8,128)(2,1)S(1)} %pad.9), channel_id=2, replica_groups=mesh['z'=16,'y_lo'=2,'core'=2,'y_hi'=2,'x'=4] {'core'}, dimensions={0}, use_global_device_ids=true | all-gather | bytes 36864 | tf_op jit(solution)/shard_map/all_gather | solution.py:21
  13.5 3.3 %all-gather.1 = bf16[4,16,384]{2,1,0:T(8,128)(2,1)S(1)} all-gather(bf16[2,16,384]{2,1,0:T(8,128)(2,1)S(1)} %bitcast.78), channel_id=3, replica_groups=mesh['z'=16,'y_lo'=2,'core'=2,'y_hi'=2,'x'=4] {'y_lo'}, dimensions={0}, use_global_device_ids=true | all-gather | bytes 73728 | tf_op jit(solution)/shard_map/all_gather | solution.py:22
  16.9 28.0 %all-gather.2 = bf16[32,2,16,384]{3,2,1,0:T(8,128)(2,1)S(1)} all-gather(bf16[2,2,16,384]{3,2,1,0:T(8,128)(2,1)S(1)} %bitcast.75), channel_id=4, replica_groups=mesh['z'=16,'y_lo'=2,'core'=2,'y_hi'=2,'x'=4] {'z'}, dimensions={0}, use_global_device_ids=true | all-gather | bytes 835584 | tf_op jit(solution)/shard_map/all_gather | solution.py:23
  45.8 0.8 fusion.5
  47.4 0.4 convolution_convert_fusion.3
  48.1 21.5 %all_to_all.15 = bf16[8,128,768]{1,2,0:T(8,128)(2,1)S(1)} all-to-all(bf16[8,128,768]{1,2,0:T(8,128)(2,1)S(1)} %copy_bitcast_fusion), channel_id=1, replica_groups=mesh['z'=16,'y_lo'=2,'core'=2,'y_hi'=2,'x'=4] {'y_hi','x'}, dimensions={0} | all-to-all | bytes 3145728 | tf_op jit(solution)/shard_map/all_to_all | solution.py:63
  70.2 0.7 copy-done.1
  71.4 0.4 multiply_convert_fusion.1
  72.5 1.3 copy.45
  73.8 4.3 %all-to-all-start.1 = ((f32[8,128,384]{2,1,0:T(8,128)}), f32[8,128,384]{2,1,0:T(8,128)}, u32[]{:S(2)}, u32[]{:S(2)}) async-start(f32[8,128,384]{2,1,0:T(8,128)} %bitcast.68), calls=%async_computation.1 | async-start | bytes 3145728 | tf_op jit(solution)/shard_map/all_to_all | solution.py:85
  78.3 14.6 %all-to-all-done.1 = f32[8,128,384]{2,1,0:T(8,128)} async-done(((f32[8,128,384]{2,1,0:T(8,128)}), f32[8,128,384]{2,1,0:T(8,128)}, u32[]{:S(2)}, u32[]{:S(2)}) %all-to-all-start.1) | async-done | bytes 1572896 | tf_op jit(solution)/shard_map/all_to_all | solution.py:85
  92.9 2.5 %fusion.8 = f32[64,4,384]{2,0,1:T(8,128)S(1)} fusion(f32[1024,384,1]{1,0,2:T(8,128)} %bitcast.15, pred[64,4,1024]{2,1,0:T(4,128)(4,1)S(1)} %dot_general.35), kind=kOutput, calls=%fused_computation.19 | convolution fusion | flops 1207959552 | bytes 2228224 | tf_op jit(solution)/shard_map/dot_general | solution.py:86
  95.4 1.0 copy.38
  96.4 17.6 %all-to-all-start.2 = ((f32[64,4,384]{2,1,0:T(4,128)}), f32[64,4,384]{2,1,0:T(4,128)S(1)}, u32[]{:S(2)}, u32[]{:S(2)}) async-start(f32[64,4,384]{2,1,0:T(4,128)} %copy.38), calls=%async_computation.2 | async-start | bytes 786432 | tf_op jit(solution)/shard_map/all_to_all | solution.py:89
  113.9 1.2 fusion
  115.2 1.2 fusion.1
  116.4 1.3 fusion.2
  117.7 24.2 %all-to-all-done.2 = f32[64,4,384]{2,1,0:T(4,128)S(1)} async-done(((f32[64,4,384]{2,1,0:T(4,128)}), f32[64,4,384]{2,1,0:T(4,128)S(1)}, u32[]{:S(2)}, u32[]{:S(2)}) %all-to-all-start.2) | async-done | bytes 393248 | tf_op jit(solution)/shard_map/all_to_all | solution.py:89
  141.8 0.7 reduce_sum.25
  (38 shorter events, 4.2 us)
Async XLA Ops:
  0.6 69.2 %copy-start = (bf16[1,3072,128]{2,1,0:T(8,128)(2,1)S(1)}, bf16[1,3072,128]{2,1,0:T(8,128)(2,1)}, u32[]{:S(2)}) copy-start(bf16[1,3072,128]{2,1,0:T(8,128)(2,1)} %param.13) | copy-start | bytes 2359300
  69.8 1.1 copy-start.1
  69.8 1.5 %copy-start.2 = (bf16[1,128,3072]{2,1,0:T(8,128)(2,1)S(1)}, bf16[1,128,3072]{2,1,0:T(8,128)(2,1)}, u32[]{:S(2)}) copy-start(bf16[1,128,3072]{2,1,0:T(8,128)(2,1)} %param.15) | copy-start | bytes 2359300
  73.8 19.1 %all-to-all-start.1 = ((f32[8,128,384]{2,1,0:T(8,128)}), f32[8,128,384]{2,1,0:T(8,128)}, u32[]{:S(2)}, u32[]{:S(2)}) async-start(f32[8,128,384]{2,1,0:T(8,128)} %bitcast.68), calls=%async_computation.1 | async-start | bytes 3145728 | tf_op jit(solution)/shard_map/all_to_all | solution.py:85
  96.4 45.5 %all-to-all-start.2 = ((f32[64,4,384]{2,1,0:T(4,128)}), f32[64,4,384]{2,1,0:T(4,128)S(1)}, u32[]{:S(2)}, u32[]{:S(2)}) async-start(f32[64,4,384]{2,1,0:T(4,128)} %copy.38), calls=%async_computation.2 | async-start | bytes 786432 | tf_op jit(solution)/shard_map/all_to_all | solution.py:89

commit v2 on v1

v2 whole, which is shorter than its diff:
```python
import jax
import jax.numpy as jnp
from jax import lax
from jax.sharding import Mesh, PartitionSpec as P

MOST = 2
DP = ("z", "y_lo", "core")
EX = ("y_hi", "x")
CLASS = ("y_lo", "core")
LOCAL = CLASS + EX


def forward_part(rows_in, w_gate, w_up):
    gate_pre = jnp.dot(rows_in, w_gate, preferred_element_type=jnp.float32)
    up_pre = jnp.dot(rows_in, w_up, preferred_element_type=jnp.float32)
    gate_sig = jax.nn.sigmoid(gate_pre)
    activated = gate_pre * gate_sig
    hidden = (activated * up_pre).astype(jnp.bfloat16)
    return (gate_pre, up_pre, gate_sig, activated, hidden)


def per_device(inputs, routes, combine, cotangent, w_gate, w_up, w_down):
    tok = inputs.shape[0]
    width_part = inputs.shape[1]
    n_ex = lax.axis_size(EX)
    n_z = lax.axis_size("z")
    n_class = lax.axis_size(CLASS)
    per_class = n_z * MOST
    capacity = n_class * per_class
    slots_in_block = 2 * tok

    scaled = (
        combine.reshape(-1)[:, None] * jnp.repeat(cotangent, 2, axis=0).astype(jnp.float32)
    ).astype(jnp.bfloat16)
    route_row = jnp.zeros((1, width_part), jnp.bfloat16)
    route_row = route_row.at[0, :slots_in_block].set(routes.reshape(-1).astype(jnp.bfloat16))
    packed = jnp.concatenate([inputs, scaled, route_row], axis=0)
    pad_rows = (-packed.shape[0]) % 16
    packed = jnp.pad(packed, ((0, pad_rows), (0, 0)))
    every = lax.all_gather(packed, "z", axis=0)
    class_in = every[:, :tok, :].reshape(n_z * tok, width_part)
    class_scaled = every[:, tok : 3 * tok, :].reshape(n_z * slots_in_block, width_part)
    class_routes = every[:, 3 * tok, :slots_in_block].astype(jnp.int32)

    onehot = (class_routes[:, :, None] == jnp.arange(n_ex, dtype=jnp.int32)).astype(jnp.int32)
    before = jnp.cumsum(onehot, axis=1) - onehot
    rank = jnp.sum(before * onehot, axis=2)
    block_id = jnp.arange(n_z, dtype=jnp.int32)[:, None]
    column = (class_routes * per_class + block_id * MOST + rank).reshape(-1)
    placer = column[:, None] == jnp.arange(n_ex * per_class, dtype=jnp.int32)[None, :]
    placer_tok = jnp.any(placer.reshape(n_z * tok, 2, n_ex * per_class), axis=1)

    sent_in = jnp.dot(
        placer_tok.astype(jnp.bfloat16).T, class_in, preferred_element_type=jnp.float32
    ).astype(jnp.bfloat16)
    sent_grad = jnp.dot(
        placer.astype(jnp.bfloat16).T, class_scaled, preferred_element_type=jnp.float32
    ).astype(jnp.bfloat16)
    sent = jnp.concatenate([sent_in, sent_grad], axis=1).reshape(n_ex, per_class, 2 * width_part)
    sent = jnp.broadcast_to(sent[None], (n_class,) + sent.shape)
    sent = sent.reshape(n_class * n_ex, per_class, 2 * width_part)
    got = lax.all_to_all(sent, LOCAL, 0, 0, tiled=True)
    got = got.reshape(n_class, n_ex, per_class, 2, width_part).transpose(3, 0, 2, 1, 4)
    rows_in = got[0].reshape(capacity, n_ex * width_part)
    rows_grad = got[1].reshape(capacity, n_ex * width_part)

    gate_w, up_w, down_w = w_gate[0], w_up[0], w_down[0]
    gate_pre, up_pre, gate_sig, activated, hidden = forward_part(rows_in, gate_w, up_w)
    hidden_delta = jnp.dot(rows_grad, down_w.T, preferred_element_type=jnp.float32)
    down_grad = jnp.dot(hidden.T, rows_grad, preferred_element_type=jnp.float32).astype(
        jnp.bfloat16
    )
    gate_delta = (hidden_delta * up_pre * gate_sig * (1.0 + gate_pre * (1.0 - gate_sig))).astype(
        jnp.bfloat16
    )
    up_delta = (hidden_delta * activated).astype(jnp.bfloat16)
    gate_grad = jnp.dot(rows_in.T, gate_delta, preferred_element_type=jnp.float32).astype(
        jnp.bfloat16
    )
    up_grad = jnp.dot(rows_in.T, up_delta, preferred_element_type=jnp.float32).astype(jnp.bfloat16)
    from_gate = jnp.dot(gate_delta, gate_w.T, preferred_element_type=jnp.float32)
    from_up = jnp.dot(up_delta, up_w.T, preferred_element_type=jnp.float32)
    partial = (from_gate + from_up).reshape(n_class, per_class, n_ex, width_part)
    partial = partial.transpose(0, 2, 1, 3).reshape(n_class * n_ex, per_class, width_part)
    back = lax.all_to_all(partial, LOCAL, 0, 0, tiled=True)
    back = jnp.sum(back.reshape(n_class, n_ex * per_class, width_part), axis=0)
    token_part = jnp.dot(placer_tok.astype(jnp.float32), back, precision=lax.Precision.HIGHEST)
    owned = lax.all_to_all(token_part.reshape(n_z, tok, width_part), "z", 0, 0, tiled=True)
    input_grad = jnp.sum(owned, axis=0).astype(jnp.bfloat16)
    return (input_grad, gate_grad[None], up_grad[None], down_grad[None])


def solution(mesh):
    n_dp, n_ex = mesh.shape["dp"], mesh.shape["expert"]
    fine = Mesh(mesh.devices.reshape(n_dp // 4, 2, 2, 2, n_ex // 2), DP + EX)
    placed = (
        P(DP, EX),
        P(DP, None),
        P(DP, None),
        P(DP, EX),
        P(EX, None, DP),
        P(EX, None, DP),
        P(EX, DP, None),
    )
    return jax.shard_map(
        per_device,
        mesh=fine,
        in_specs=placed,
        out_specs=(
            P(DP, EX),
            P(EX, None, DP),
            P(EX, None, DP),
            P(EX, DP, None),
        ),
        check_vma=False,
    )
```

time: 143 us -> 139 us (0.972)
  starting transfers between devices: 21.9 us -> 12.1 us
  local copies, waits for them, and re-layouts: 6.06 us -> 14.9 us
  waiting for transfers between devices: 38.7 us -> 30.2 us
  blocking collectives: 61.3 us -> 67.3 us
  matrix products: 9.45 us -> 6.56 us
    all_to_all x1, blocking collectives: 21.5 us -> 37.1 us  [per_device(): got = lax.all_to_all(sent, LOCAL, 0, 0, tiled=True)]
    all_to_all x2, starting transfers between devices: 21.9 us -> 12.1 us  [the longest x1 6.44 us: per_device(): lax.all_to_all(token_part.reshape(n_z, tok, width_part), 'z', 0, 0, tiled...]
    all_gather x3 -> x1, blocking collectives: 39.7 us -> 30.2 us  [per_device(): every = lax.all_gather(packed, 'z', axis=0)]
    all_to_all x2, waiting for transfers between devices: 38.7 us -> 30.2 us  [the longest x1 22.1 us: per_device(): back = lax.all_to_all(partial, LOCAL, 0, 0, tiled=True)]
    slice x1 -> x2, local copies, waits for them, and re-layouts: 0.1 us -> 4.39 us  [per_device(): rows_grad = got[1].reshape(capacity, n_ex * width_part)]
    reshape x2 -> x3, local copies, waits for them, and re-layouts: 1.3 us -> 4.84 us  [the longest x1 3.39 us: per_device(): got.reshape(n_class, n_ex, per_class, 2, width_part)]
    dot_general x1, matrix products: 2.52 us -> 0.28 us  [per_device(): jnp.dot(placer_tok.astype(jnp.float32), back, precision=lax.Precision.HIG...]
    reduce_sum x0 -> x1, other arithmetic: none -> 1.53 us  [per_device(): back = jnp.sum(back.reshape(n_class, n_ex * per_class, width_part), axis=0)]
where the time goes in v2:
time: 139 us; the launch traced here: 137 us
  blocking collectives  67.3 us (48%)
  waiting for transfers between devices  30.2 us (22%)
  local copies, waits for them, and re-layouts  14.9 us (11%)
  starting transfers between devices  12.1 us (9%)
  matrix products  6.56 us (5%)
  other arithmetic  5.19 us (4%)
    all_to_all x1, blocking collectives, per_device(): got = lax.all_to_all(sent, LOCAL, 0, 0, tiled=True)  37.1 us
    all_gather x1, blocking collectives, per_device(): every = lax.all_gather(packed, 'z', axis=0)  30.2 us
    all_to_all x1, waiting for transfers between devices, per_device(): back = lax.all_to_all(partial, LOCAL, 0, 0, tiled=True)  22.1 us
    all_to_all x1, waiting for transfers between devices, per_device(): lax.all_to_all(token_part.reshape(n_z, tok, width_part), 'z', 0, 0, tiled...  8.04 us
    all_to_all x1, starting transfers between devices, per_device(): lax.all_to_all(token_part.reshape(n_z, tok, width_part), 'z', 0, 0, tiled...  6.44 us
    all_to_all x1, starting transfers between devices, per_device(): back = lax.all_to_all(partial, LOCAL, 0, 0, tiled=True)  5.69 us
    slice x2, local copies, waits for them, and re-layouts, per_device(): rows_grad = got[1].reshape(capacity, n_ex * width_part)  4.39 us
    reshape x1, local copies, waits for them, and re-layouts, per_device(): got.reshape(n_class, n_ex, per_class, 2, width_part)  3.39 us
  transfers between devices with their start and end apart: 2, of which 2 were waited for; matrix products, arithmetic and copies ran while one was open for 3% of the time, Pallas kernels for 0%

profile of v2, /device:TPU:1, one launch (start us, length us, event | category | flops | bytes accessed | tf_op | source)
XLA Modules:
  0.0 137.1 jit_solution(878779209676148167)
XLA Ops:
  0.6 0.6 compare_reduce_fusion
  1.3 1.3 broadcast_select_fusion
  2.8 0.7 broadcast_in_dim.24
  3.5 0.8 copy.39
  4.4 0.7 fusion.22
  5.2 30.2 %all-gather = bf16[256,384]{1,0:T(8,128)(2,1)S(1)} all-gather(bf16[16,384]{1,0:T(8,128)(2,1)S(1)} %pad.9), channel_id=2, replica_groups=mesh['z'=16,'y_lo'=2,'core'=2,'y_hi'=2,'x'=4] {'z'}, dimensions={0}, use_global_device_ids=true | all-gather | bytes 208896 | tf_op jit(solution)/shard_map/all_gather | solution.py:40
  37.4 37.1 %all_to_all.15 = bf16[32,32,768]{2,1,0:T(8,128)(2,1)} all-to-all(bf16[32,32,768]{2,1,0:T(8,128)(2,1)S(1)} %bitcast.69), channel_id=1, replica_groups=mesh['z'=16,'y_lo'=2,'core'=2,'y_hi'=2,'x'=4] {'y_lo','core','y_hi','x'}, dimensions={0} | all-to-all | bytes 3145728 | tf_op jit(solution)/shard_map/all_to_all | solution.py:62
  74.5 3.4 %reshape.132 = bf16[4,8,32,2,384]{4,3,2,1,0:T(2,128)(2,1)S(1)} reshape(bf16[32,32,768]{2,1,0:T(8,128)(2,1)} %all_to_all.15) | data formatting | bytes 3145728 | tf_op jit(solution)/shard_map/reshape | solution.py:63
  77.9 3.5 %fusion.26 = (bf16[1,4,32,8,384]{4,0,2,3,1:T(2,128)(2,1)S(1)}, bf16[1,4,32,8,384]{4,0,2,3,1:T(2,128)(2,1)S(1)}) fusion(bf16[2,4,32,8,384]{4,0,2,3,1:T(2,128)(2,1)S(1)} %bitcast.64), kind=kLoop, calls=%fused_computation.51 | loop fusion | bytes 3145728 | tf_op jit(solution)/shard_map/slice | solution.py:65
  81.4 0.9 copy.46
  82.8 0.6 copy-done.1
  83.8 0.9 copy.45
  85.0 0.4 multiply_convert_fusion.1
  86.4 1.4 %copy.47 = f32[4,32,8,384]{3,1,2,0:T(8,128)} copy(f32[4,32,8,384]{3,2,1,0:T(8,128)S(1)} %bitcast.68) | data formatting | bytes 3145728 | tf_op jit(solution)/shard_map/reshape | solution.py:83
  87.8 5.7 %all-to-all-start.1 = ((f32[32,32,384]{2,1,0:T(8,128)}), f32[32,32,384]{2,1,0:T(8,128)}, u32[]{:S(2)}, u32[]{:S(2)}) async-start(f32[32,32,384]{2,1,0:T(8,128)} %bitcast.67), calls=%async_computation.1 | async-start | bytes 3145728 | tf_op jit(solution)/shard_map/all_to_all | solution.py:85
  93.5 22.1 %all-to-all-done.1 = f32[32,32,384]{2,1,0:T(8,128)} async-done(((f32[32,32,384]{2,1,0:T(8,128)}), f32[32,32,384]{2,1,0:T(8,128)}, u32[]{:S(2)}, u32[]{:S(2)}) %all-to-all-start.1) | async-done | bytes 1572896 | tf_op jit(solution)/shard_map/all_to_all | solution.py:85
  115.7 1.5 %bitcast_reduce_fusion = f32[256,384]{1,0:T(8,128)S(1)} fusion(f32[4,256,384]{2,1,0:T(8,128)} %bitcast.59), kind=kLoop, calls=%fused_computation.7 | loop fusion | flops 294912 | bytes 1966080 | tf_op jit(solution)/shard_map/reduce_sum | solution.py:86
  117.5 0.7 copy.49
  118.1 6.4 %all-to-all-start.2 = ((f32[16,4,384]{2,1,0:T(4,128)}), f32[16,4,384]{2,1,0:T(4,128)S(1)}, u32[]{:S(2)}, u32[]{:S(2)}) async-start(f32[16,4,384]{2,1,0:T(4,128)} %copy.49), calls=%async_computation.2 | async-start | bytes 196608 | tf_op jit(solution)/shard_map/all_to_all | solution.py:88
  124.6 1.3 fusion
  125.9 1.3 fusion.1
  127.2 1.3 fusion.2
  128.5 8.0 %all-to-all-done.2 = f32[16,4,384]{2,1,0:T(4,128)S(1)} async-done(((f32[16,4,384]{2,1,0:T(4,128)}), f32[16,4,384]{2,1,0:T(4,128)S(1)}, u32[]{:S(2)}, u32[]{:S(2)}) %all-to-all-start.2) | async-done | bytes 98336 | tf_op jit(solution)/shard_map/all_to_all | solution.py:88
  136.5 0.6 reduce_sum.35
  (44 shorter events, 4.8 us)
Async XLA Ops:
  0.6 81.8 %copy-start = (bf16[1,3072,128]{2,1,0:T(8,128)(2,1)S(1)}, bf16[1,3072,128]{2,1,0:T(8,128)(2,1)}, u32[]{:S(2)}) copy-start(bf16[1,3072,128]{2,1,0:T(8,128)(2,1)} %param.13) | copy-start | bytes 2359300
  82.3 1.1 copy-start.1
  83.8 1.1 copy-start.2
  87.8 27.9 %all-to-all-start.1 = ((f32[32,32,384]{2,1,0:T(8,128)}), f32[32,32,384]{2,1,0:T(8,128)}, u32[]{:S(2)}, u32[]{:S(2)}) async-start(f32[32,32,384]{2,1,0:T(8,128)} %bitcast.67), calls=%async_computation.1 | async-start | bytes 3145728 | tf_op jit(solution)/shard_map/all_to_all | solution.py:85
  118.1 18.4 %all-to-all-start.2 = ((f32[16,4,384]{2,1,0:T(4,128)}), f32[16,4,384]{2,1,0:T(4,128)S(1)}, u32[]{:S(2)}, u32[]{:S(2)}) async-start(f32[16,4,384]{2,1,0:T(4,128)} %copy.49), calls=%async_computation.2 | async-start | bytes 196608 | tf_op jit(solution)/shard_map/all_to_all | solution.py:88

commit v3 on v2

--- a/solution.py
+++ b/solution.py
@@ -37,7 +37,8 @@
     packed = jnp.concatenate([inputs, scaled, route_row], axis=0)
     pad_rows = (-packed.shape[0]) % 16
     packed = jnp.pad(packed, ((0, pad_rows), (0, 0)))
-    every = lax.all_gather(packed, "z", axis=0)
+    every = jnp.broadcast_to(packed[None], (n_z,) + packed.shape)
+    every = lax.all_to_all(every, "z", 0, 0, tiled=True)
     class_in = every[:, :tok, :].reshape(n_z * tok, width_part)
     class_scaled = every[:, tok : 3 * tok, :].reshape(n_z * slots_in_block, width_part)
     class_routes = every[:, 3 * tok, :slots_in_block].astype(jnp.int32)

time: 139 us -> 133 us (0.957)
  blocking collectives: 67.3 us -> 34.2 us
  starting transfers between devices: 12.1 us -> 26.1 us
  waiting for transfers between devices: 30.2 us -> 42.4 us
    all_gather x1 -> x0, blocking collectives: 30.2 us -> none  [per_device(): every = lax.all_gather(packed, 'z', axis=0)]
    all_to_all x0 -> x1, starting transfers between devices: none -> 15.7 us  [per_device(): every = lax.all_to_all(every, 'z', 0, 0, tiled=True)]
    all_to_all x0 -> x1, waiting for transfers between devices: none -> 12.2 us  [per_device(): every = lax.all_to_all(every, 'z', 0, 0, tiled=True)]
    all_to_all x1, blocking collectives: 37.1 us -> 34.2 us  [per_device(): got = lax.all_to_all(sent, LOCAL, 0, 0, tiled=True)]
    all_to_all x1, starting transfers between devices: 6.44 us -> 4.63 us  [per_device(): lax.all_to_all(token_part.reshape(n_z, tok, width_part), 'z', 0, 0, tiled...]
  transfers between devices with their start and end apart: 2 -> 3, of which waited for: 2 -> 3; matrix products, arithmetic and copies ran while one was open for 3% -> 3% of each run, Pallas kernels for 0% -> 0%
where the time goes in v3:
time: 133 us; the launch traced here: 131 us
  waiting for transfers between devices  42.4 us (32%)
  blocking collectives  34.2 us (26%)
  starting transfers between devices  26.1 us (20%)
  local copies, waits for them, and re-layouts  15.7 us (12%)
  matrix products  6.57 us (5%)
  other arithmetic  5.14 us (4%)
    all_to_all x1, blocking collectives, per_device(): got = lax.all_to_all(sent, LOCAL, 0, 0, tiled=True)  34.2 us
    all_to_all x1, waiting for transfers between devices, per_device(): back = lax.all_to_all(partial, LOCAL, 0, 0, tiled=True)  22.1 us
    all_to_all x1, starting transfers between devices, per_device(): every = lax.all_to_all(every, 'z', 0, 0, tiled=True)  15.7 us
    all_to_all x1, waiting for transfers between devices, per_device(): every = lax.all_to_all(every, 'z', 0, 0, tiled=True)  12.2 us
    all_to_all x1, waiting for transfers between devices, per_device(): lax.all_to_all(token_part.reshape(n_z, tok, width_part), 'z', 0, 0, tiled...  8.03 us
    all_to_all x1, starting transfers between devices, per_device(): back = lax.all_to_all(partial, LOCAL, 0, 0, tiled=True)  5.68 us
    all_to_all x1, starting transfers between devices, per_device(): lax.all_to_all(token_part.reshape(n_z, tok, width_part), 'z', 0, 0, tiled...  4.63 us
    slice x2, local copies, waits for them, and re-layouts, per_device(): rows_grad = got[1].reshape(capacity, n_ex * width_part)  4.39 us
  transfers between devices with their start and end apart: 3, of which 3 were waited for; matrix products, arithmetic and copies ran while one was open for 3% of the time, Pallas kernels for 0%

profile of v3, /device:TPU:1, one launch (start us, length us, event | category | flops | bytes accessed | tf_op | source)
XLA Modules:
  0.0 130.9 jit_solution(9709307512845933559)
XLA Ops:
  0.6 0.6 compare_reduce_fusion
  1.3 1.3 %broadcast_select_fusion = bf16[4,2]{0,1:T(2,128)(2,1)S(1)} fusion(pred[]{:T(512)} %compare_reduce_fusion, s32[4,2]{0,1:T(2,128)} %param.10), kind=kLoop, calls=%fused_computation.46 | loop fusion | flops 16 | bytes 49 | tf_op jit(solution)/shard_map/select.9
  2.8 0.7 broadcast_in_dim.14
  3.5 0.8 copy.47
  4.4 0.7 fusion.22
  5.2 0.7 broadcast_in_dim.15
  5.9 15.7 %all-to-all-start = ((bf16[16,16,384]{2,1,0:T(8,128)(2,1)}), bf16[16,16,384]{2,1,0:T(8,128)(2,1)S(1)}, u32[]{:S(2)}, u32[]{:S(2)}) async-start(bf16[16,16,384]{2,1,0:T(8,128)(2,1)} %broadcast_in_dim.15), calls=%async_computation | async-start | bytes 393216 | tf_op jit(solution)/shard_map/all_to_all | solution.py:41
  21.9 12.2 %all-to-all-done = bf16[16,16,384]{2,1,0:T(8,128)(2,1)S(1)} async-done(((bf16[16,16,384]{2,1,0:T(8,128)(2,1)}), bf16[16,16,384]{2,1,0:T(8,128)(2,1)S(1)}, u32[]{:S(2)}, u32[]{:S(2)}) %all-to-all-start) | async-done | bytes 196640 | tf_op jit(solution)/shard_map/all_to_all | solution.py:41
  35.9 34.2 %all_to_all.20 = bf16[32,32,768]{2,1,0:T(8,128)(2,1)} all-to-all(bf16[32,32,768]{2,1,0:T(8,128)(2,1)S(1)} %bitcast.72), channel_id=1, replica_groups=mesh['z'=16,'y_lo'=2,'core'=2,'y_hi'=2,'x'=4] {'y_lo','core','y_hi','x'}, dimensions={0} | all-to-all | bytes 3145728 | tf_op jit(solution)/shard_map/all_to_all | solution.py:63
  70.1 3.4 %reshape.133 = bf16[4,8,32,2,384]{4,3,2,1,0:T(2,128)(2,1)S(1)} reshape(bf16[32,32,768]{2,1,0:T(8,128)(2,1)} %all_to_all.20) | data formatting | bytes 3145728 | tf_op jit(solution)/shard_map/reshape | solution.py:64
  73.5 3.5 %fusion.25 = (bf16[1,4,32,8,384]{4,0,2,3,1:T(2,128)(2,1)S(1)}, bf16[1,4,32,8,384]{4,0,2,3,1:T(2,128)(2,1)S(1)}) fusion(bf16[2,4,32,8,384]{4,0,2,3,1:T(2,128)(2,1)S(1)} %bitcast.67), kind=kLoop, calls=%fused_computation.50 | loop fusion | bytes 3145728 | tf_op jit(solution)/shard_map/slice | solution.py:66
  77.0 0.9 copy.56
  78.4 0.6 copy-done.1
  79.4 0.9 copy.55
  82.0 1.4 %copy.57 = f32[4,32,8,384]{3,1,2,0:T(8,128)} copy(f32[4,32,8,384]{3,2,1,0:T(8,128)S(1)} %bitcast.71) | data formatting | bytes 3145728 | tf_op jit(solution)/shard_map/reshape | solution.py:84
  83.4 5.7 %all-to-all-start.2 = ((f32[32,32,384]{2,1,0:T(8,128)}), f32[32,32,384]{2,1,0:T(8,128)}, u32[]{:S(2)}, u32[]{:S(2)}) async-start(f32[32,32,384]{2,1,0:T(8,128)} %bitcast.70), calls=%async_computation.2 | async-start | bytes 3145728 | tf_op jit(solution)/shard_map/all_to_all | solution.py:86
  89.1 22.1 %all-to-all-done.2 = f32[32,32,384]{2,1,0:T(8,128)} async-done(((f32[32,32,384]{2,1,0:T(8,128)}), f32[32,32,384]{2,1,0:T(8,128)}, u32[]{:S(2)}, u32[]{:S(2)}) %all-to-all-start.2) | async-done | bytes 1572896 | tf_op jit(solution)/shard_map/all_to_all | solution.py:86
  111.3 1.5 %bitcast_reduce_fusion = f32[256,384]{1,0:T(8,128)S(1)} fusion(f32[4,256,384]{2,1,0:T(8,128)} %bitcast.62), kind=kLoop, calls=%fused_computation.7 | loop fusion | flops 294912 | bytes 1966080 | tf_op jit(solution)/shard_map/reduce_sum | solution.py:87
  113.1 0.7 copy.59
  113.7 4.6 %all-to-all-start.3 = ((f32[16,4,384]{2,1,0:T(4,128)}), f32[16,4,384]{2,1,0:T(4,128)S(1)}, u32[]{:S(2)}, u32[]{:S(2)}) async-start(f32[16,4,384]{2,1,0:T(4,128)} %copy.59), calls=%async_computation.3 | async-start | bytes 196608 | tf_op jit(solution)/shard_map/all_to_all | solution.py:89
  118.4 1.3 fusion
  119.7 1.3 fusion.1
  121.0 1.3 fusion.2
  122.3 8.0 %all-to-all-done.3 = f32[16,4,384]{2,1,0:T(4,128)S(1)} async-done(((f32[16,4,384]{2,1,0:T(4,128)}), f32[16,4,384]{2,1,0:T(4,128)S(1)}, u32[]{:S(2)}, u32[]{:S(2)}) %all-to-all-start.3) | async-done | bytes 98336 | tf_op jit(solution)/shard_map/all_to_all | solution.py:89
  (48 shorter events, 5.8 us)
Async XLA Ops:
  0.6 77.4 %copy-start = (bf16[1,3072,128]{2,1,0:T(8,128)(2,1)S(1)}, bf16[1,3072,128]{2,1,0:T(8,128)(2,1)}, u32[]{:S(2)}) copy-start(bf16[1,3072,128]{2,1,0:T(8,128)(2,1)} %param.13) | copy-start | bytes 2359300
  5.9 28.3 %all-to-all-start = ((bf16[16,16,384]{2,1,0:T(8,128)(2,1)}), bf16[16,16,384]{2,1,0:T(8,128)(2,1)S(1)}, u32[]{:S(2)}, u32[]{:S(2)}) async-start(bf16[16,16,384]{2,1,0:T(8,128)(2,1)} %broadcast_in_dim.15), calls=%async_computation | async-start | bytes 393216 | tf_op jit(solution)/shard_map/all_to_all | solution.py:41
  77.9 1.1 copy-start.1
  79.4 1.1 copy-start.2
  83.4 27.9 %all-to-all-start.2 = ((f32[32,32,384]{2,1,0:T(8,128)}), f32[32,32,384]{2,1,0:T(8,128)}, u32[]{:S(2)}, u32[]{:S(2)}) async-start(f32[32,32,384]{2,1,0:T(8,128)} %bitcast.70), calls=%async_computation.2 | async-start | bytes 3145728 | tf_op jit(solution)/shard_map/all_to_all | solution.py:86
  113.7 16.6 %all-to-all-start.3 = ((f32[16,4,384]{2,1,0:T(4,128)}), f32[16,4,384]{2,1,0:T(4,128)S(1)}, u32[]{:S(2)}, u32[]{:S(2)}) async-start(f32[16,4,384]{2,1,0:T(4,128)} %copy.59), calls=%async_computation.3 | async-start | bytes 196608 | tf_op jit(solution)/shard_map/all_to_all | solution.py:89

commit v4 on v3

--- a/solution.py
+++ b/solution.py
@@ -57,11 +57,14 @@
     sent_grad = jnp.dot(
         placer.astype(jnp.bfloat16).T, class_scaled, preferred_element_type=jnp.float32
     ).astype(jnp.bfloat16)
-    sent = jnp.concatenate([sent_in, sent_grad], axis=1).reshape(n_ex, per_class, 2 * width_part)
+    sent = jnp.stack(
+        [sent_in.reshape(n_ex, per_class, width_part), sent_grad.reshape(n_ex, per_class, width_part)],
+        axis=1,
+    )
     sent = jnp.broadcast_to(sent[None], (n_class,) + sent.shape)
-    sent = sent.reshape(n_class * n_ex, per_class, 2 * width_part)
+    sent = sent.reshape(n_class * n_ex, 2, per_class, width_part)
     got = lax.all_to_all(sent, LOCAL, 0, 0, tiled=True)
-    got = got.reshape(n_class, n_ex, per_class, 2, width_part).transpose(3, 0, 2, 1, 4)
+    got = got.reshape(n_class, n_ex, 2, per_class, width_part).transpose(2, 0, 3, 1, 4)
     rows_in = got[0].reshape(capacity, n_ex * width_part)
     rows_grad = got[1].reshape(capacity, n_ex * width_part)
 

time: 133 us -> 126 us (0.947)
  local copies, waits for them, and re-layouts: 15.7 us -> 8.46 us
    slice x2, local copies, waits for them, and re-layouts: 4.39 us -> 0.48 us  [per_device(): rows_grad = got[1].reshape(capacity, n_ex * width_part)]
    reshape x1 -> x0, local copies, waits for them, and re-layouts: 3.39 us -> none  [per_device(): got.reshape(n_class, n_ex, per_class, 2, width_part)]
where the time goes in v4:
time: 126 us; the launch traced here: 124 us
  waiting for transfers between devices  42.4 us (34%)
  blocking collectives  34.1 us (27%)
  starting transfers between devices  26.1 us (21%)
  local copies, waits for them, and re-layouts  8.46 us (7%)
  matrix products  6.58 us (5%)
  other arithmetic  5.16 us (4%)
    all_to_all x1, blocking collectives, per_device(): got = lax.all_to_all(sent, LOCAL, 0, 0, tiled=True)  34.1 us
    all_to_all x1, waiting for transfers between devices, per_device(): back = lax.all_to_all(partial, LOCAL, 0, 0, tiled=True)  22.1 us
    all_to_all x1, starting transfers between devices, per_device(): every = lax.all_to_all(every, 'z', 0, 0, tiled=True)  15.7 us
    all_to_all x1, waiting for transfers between devices, per_device(): every = lax.all_to_all(every, 'z', 0, 0, tiled=True)  12.2 us
    all_to_all x1, waiting for transfers between devices, per_device(): lax.all_to_all(token_part.reshape(n_z, tok, width_part), 'z', 0, 0, tiled...  8.03 us
    all_to_all x1, starting transfers between devices, per_device(): back = lax.all_to_all(partial, LOCAL, 0, 0, tiled=True)  5.68 us
    all_to_all x1, starting transfers between devices, per_device(): lax.all_to_all(token_part.reshape(n_z, tok, width_part), 'z', 0, 0, tiled...  4.63 us
    unnamed x11, local copies, waits for them, and re-layouts  2.73 us
  transfers between devices with their start and end apart: 3, of which 3 were waited for; matrix products, arithmetic and copies ran while one was open for 3% of the time, Pallas kernels for 0%

profile of v4, /device:TPU:1, one launch (start us, length us, event | category | flops | bytes accessed | tf_op | source)
XLA Modules:
  0.0 123.6 jit_solution(4684042368240030563)
XLA Ops:
  0.6 0.6 compare_reduce_fusion
  1.3 1.3 %broadcast_select_fusion = bf16[4,2]{0,1:T(2,128)(2,1)S(1)} fusion(pred[]{:T(512)} %compare_reduce_fusion, s32[4,2]{0,1:T(2,128)} %param.10), kind=kLoop, calls=%fused_computation.46 | loop fusion | flops 16 | bytes 49 | tf_op jit(solution)/shard_map/select.9
  2.8 0.7 broadcast_in_dim.12
  3.5 0.8 copy.51
  4.4 0.7 fusion.22
  5.2 0.7 broadcast_in_dim.13
  5.9 15.7 %all-to-all-start = ((bf16[16,16,384]{2,1,0:T(8,128)(2,1)}), bf16[16,16,384]{2,1,0:T(8,128)(2,1)S(1)}, u32[]{:S(2)}, u32[]{:S(2)}) async-start(bf16[16,16,384]{2,1,0:T(8,128)(2,1)} %broadcast_in_dim.13), calls=%async_computation | async-start | bytes 393216 | tf_op jit(solution)/shard_map/all_to_all | solution.py:41
  21.9 12.2 %all-to-all-done = bf16[16,16,384]{2,1,0:T(8,128)(2,1)S(1)} async-done(((bf16[16,16,384]{2,1,0:T(8,128)(2,1)}), bf16[16,16,384]{2,1,0:T(8,128)(2,1)S(1)}, u32[]{:S(2)}, u32[]{:S(2)}) %all-to-all-start) | async-done | bytes 196640 | tf_op jit(solution)/shard_map/all_to_all | solution.py:41
  36.1 34.1 %all_to_all.20 = bf16[32,2,32,384]{3,2,1,0:T(8,128)(2,1)S(1)} all-to-all(bf16[32,2,32,384]{3,2,1,0:T(8,128)(2,1)S(1)} %bitcast.75), channel_id=1, replica_groups=mesh['z'=16,'y_lo'=2,'core'=2,'y_hi'=2,'x'=4] {'y_lo','core','y_hi','x'}, dimensions={0} | all-to-all | bytes 3145728 | tf_op jit(solution)/shard_map/all_to_all | solution.py:66
  71.2 0.6 copy-done.1
  72.6 0.7 copy-done.2
  73.3 0.4 multiply_convert_fusion.1
  74.0 0.4 convolution_add_fusion
  74.7 1.4 %copy.62 = f32[4,32,8,384]{3,1,2,0:T(8,128)} copy(f32[4,32,8,384]{3,2,1,0:T(8,128)S(1)} %bitcast.74) | data formatting | bytes 3145728 | tf_op jit(solution)/shard_map/reshape | solution.py:87
  76.1 5.7 %all-to-all-start.2 = ((f32[32,32,384]{2,1,0:T(8,128)}), f32[32,32,384]{2,1,0:T(8,128)}, u32[]{:S(2)}, u32[]{:S(2)}) async-start(f32[32,32,384]{2,1,0:T(8,128)} %bitcast.72), calls=%async_computation.2 | async-start | bytes 3145728 | tf_op jit(solution)/shard_map/all_to_all | solution.py:89
  81.8 22.1 %all-to-all-done.2 = f32[32,32,384]{2,1,0:T(8,128)} async-done(((f32[32,32,384]{2,1,0:T(8,128)}), f32[32,32,384]{2,1,0:T(8,128)}, u32[]{:S(2)}, u32[]{:S(2)}) %all-to-all-start.2) | async-done | bytes 1572896 | tf_op jit(solution)/shard_map/all_to_all | solution.py:89
  104.0 1.5 %bitcast_reduce_fusion = f32[256,384]{1,0:T(8,128)S(1)} fusion(f32[4,256,384]{2,1,0:T(8,128)} %bitcast.65), kind=kLoop, calls=%fused_computation.7 | loop fusion | flops 294912 | bytes 1966080 | tf_op jit(solution)/shard_map/reduce_sum | solution.py:90
  105.8 0.7 copy.64
  106.5 4.6 %all-to-all-start.3 = ((f32[16,4,384]{2,1,0:T(4,128)}), f32[16,4,384]{2,1,0:T(4,128)S(1)}, u32[]{:S(2)}, u32[]{:S(2)}) async-start(f32[16,4,384]{2,1,0:T(4,128)} %copy.64), calls=%async_computation.3 | async-start | bytes 196608 | tf_op jit(solution)/shard_map/all_to_all | solution.py:92
  111.1 1.3 %fusion = bf16[1,3072,128]{2,1,0:T(8,128)(2,1)} fusion(bf16[128,3072]{1,0:T(8,128)(2,1)S(1)} %bitcast.68, bf16[128,128]{1,0:T(8,128)(2,1)S(1)} %get-tuple-element.19), kind=kOutput, calls=%fused_computation.4 | convolution fusion | flops 101056512 | bytes 1605632 | tf_op jit(solution)/shard_map/dot_general | solution.py:81
  112.4 1.3 %fusion.1 = bf16[1,3072,128]{2,1,0:T(8,128)(2,1)} fusion(bf16[128,3072]{1,0:T(8,128)(2,1)S(1)} %bitcast.69, bf16[128,128]{1,0:T(8,128)(2,1)S(1)} %get-tuple-element.18), kind=kOutput, calls=%fused_computation.5 | convolution fusion | flops 101056512 | bytes 1605632 | tf_op jit(solution)/shard_map/dot_general | solution.py:84
  113.7 1.3 %fusion.2 = bf16[1,128,3072]{2,1,0:T(8,128)(2,1)} fusion(bf16[128,3072]{1,0:T(8,128)(2,1)S(1)} %bitcast.71, f32[128,128]{1,0:T(8,128)S(1)} %fusion.9, f32[128,128]{1,0:T(8,128)S(1)} %fusion.6), kind=kOutput, calls=%fused_computation.6 | convolution fusion | flops 101154816 | bytes 1703936 | tf_op jit(solution)/shard_map/dot_general | solution.py:74
  115.0 8.0 %all-to-all-done.3 = f32[16,4,384]{2,1,0:T(4,128)S(1)} async-done(((f32[16,4,384]{2,1,0:T(4,128)}), f32[16,4,384]{2,1,0:T(4,128)S(1)}, u32[]{:S(2)}, u32[]{:S(2)}) %all-to-all-start.3) | async-done | bytes 98336 | tf_op jit(solution)/shard_map/all_to_all | solution.py:92
  123.0 0.6 reduce_sum.35
  (48 shorter events, 5.2 us)
Async XLA Ops:
  0.6 70.2 %copy-start = (bf16[1,3072,128]{2,1,0:T(8,128)(2,1)S(1)}, bf16[1,3072,128]{2,1,0:T(8,128)(2,1)}, u32[]{:S(2)}) copy-start(bf16[1,3072,128]{2,1,0:T(8,128)(2,1)} %param.13) | copy-start | bytes 2359300
  5.9 28.3 %all-to-all-start = ((bf16[16,16,384]{2,1,0:T(8,128)(2,1)}), bf16[16,16,384]{2,1,0:T(8,128)(2,1)S(1)}, u32[]{:S(2)}, u32[]{:S(2)}) async-start(bf16[16,16,384]{2,1,0:T(8,128)(2,1)} %broadcast_in_dim.13), calls=%async_computation | async-start | bytes 393216 | tf_op jit(solution)/shard_map/all_to_all | solution.py:41
  70.6 1.1 copy-start.1
  72.1 1.1 copy-start.2
  76.1 27.9 %all-to-all-start.2 = ((f32[32,32,384]{2,1,0:T(8,128)}), f32[32,32,384]{2,1,0:T(8,128)}, u32[]{:S(2)}, u32[]{:S(2)}) async-start(f32[32,32,384]{2,1,0:T(8,128)} %bitcast.72), calls=%async_computation.2 | async-start | bytes 3145728 | tf_op jit(solution)/shard_map/all_to_all | solution.py:89
  106.5 16.5 %all-to-all-start.3 = ((f32[16,4,384]{2,1,0:T(4,128)}), f32[16,4,384]{2,1,0:T(4,128)S(1)}, u32[]{:S(2)}, u32[]{:S(2)}) async-start(f32[16,4,384]{2,1,0:T(4,128)} %copy.64), calls=%async_computation.3 | async-start | bytes 196608 | tf_op jit(solution)/shard_map/all_to_all | solution.py:92

commit v5 on v4

--- a/solution.py
+++ b/solution.py
@@ -29,14 +29,14 @@
     capacity = n_class * per_class
     slots_in_block = 2 * tok
 
-    scaled = (
-        combine.reshape(-1)[:, None] * jnp.repeat(cotangent, 2, axis=0).astype(jnp.float32)
-    ).astype(jnp.bfloat16)
-    route_row = jnp.zeros((1, width_part), jnp.bfloat16)
-    route_row = route_row.at[0, :slots_in_block].set(routes.reshape(-1).astype(jnp.bfloat16))
-    packed = jnp.concatenate([inputs, scaled, route_row], axis=0)
-    pad_rows = (-packed.shape[0]) % 16
-    packed = jnp.pad(packed, ((0, pad_rows), (0, 0)))
+    scaled = (combine[:, :, None] * cotangent[:, None, :].astype(jnp.float32)).astype(jnp.bfloat16)
+    scaled = scaled.reshape(slots_in_block, width_part)
+    route_row = routes.reshape(1, slots_in_block).astype(jnp.bfloat16)
+    route_row = jnp.pad(route_row, ((0, 0), (0, width_part - slots_in_block)))
+    pad_rows = (-(3 * tok + 1)) % 16
+    packed = jnp.concatenate(
+        [inputs, scaled, route_row, jnp.zeros((pad_rows, width_part), jnp.bfloat16)], axis=0
+    )
     every = jnp.broadcast_to(packed[None], (n_z,) + packed.shape)
     every = lax.all_to_all(every, "z", 0, 0, tiled=True)
     class_in = every[:, :tok, :].reshape(n_z * tok, width_part)
@@ -82,13 +82,24 @@
         jnp.bfloat16
     )
     up_grad = jnp.dot(rows_in.T, up_delta, preferred_element_type=jnp.float32).astype(jnp.bfloat16)
-    from_gate = jnp.dot(gate_delta, gate_w.T, preferred_element_type=jnp.float32)
-    from_up = jnp.dot(up_delta, up_w.T, preferred_element_type=jnp.float32)
-    partial = (from_gate + from_up).reshape(n_class, per_class, n_ex, width_part)
-    partial = partial.transpose(0, 2, 1, 3).reshape(n_class * n_ex, per_class, width_part)
+    by_slice = (n_ex, width_part, gate_w.shape[1])
+    from_gate = jnp.einsum(
+        "csf,edf->cesd",
+        gate_delta.reshape(n_class, per_class, -1),
+        gate_w.reshape(by_slice),
+        preferred_element_type=jnp.float32,
+    )
+    from_up = jnp.einsum(
+        "csf,edf->cesd",
+        up_delta.reshape(n_class, per_class, -1),
+        up_w.reshape(by_slice),
+        preferred_element_type=jnp.float32,
+    )
+    partial = (from_gate + from_up).reshape(n_class * n_ex, per_class, width_part)
     back = lax.all_to_all(partial, LOCAL, 0, 0, tiled=True)
-    back = jnp.sum(back.reshape(n_class, n_ex * per_class, width_part), axis=0)
-    token_part = jnp.dot(placer_tok.astype(jnp.float32), back, precision=lax.Precision.HIGHEST)
+    back = back.reshape(n_class * n_ex * per_class, width_part)
+    picker = jnp.tile(placer_tok.astype(jnp.float32), (1, n_class))
+    token_part = jnp.dot(picker, back, precision=lax.Precision.HIGHEST)
     owned = lax.all_to_all(token_part.reshape(n_z, tok, width_part), "z", 0, 0, tiled=True)
     input_grad = jnp.sum(owned, axis=0).astype(jnp.bfloat16)
     return (input_grad, gate_grad[None], up_grad[None], down_grad[None])

time: 126 us -> 125 us (level)
  matrix products: 6.58 us -> 9.95 us
  other arithmetic: 5.16 us -> 2.48 us
  local copies, waits for them, and re-layouts: 8.46 us -> 7.05 us
    dot_general x3, matrix products: 1.02 us -> 4.41 us  [the longest x1 2.53 us: per_device(): token_part = jnp.dot(picker, back, precision=lax.Precision.HIGHEST)]
    another operation x2 -> x0, other arithmetic: 1.97 us -> none
    reduce_sum x1 -> x0, other arithmetic: 1.53 us -> none  [per_device(): back = jnp.sum(back.reshape(n_class, n_ex * per_class, width_part), axis=0)]
    reshape x1 -> x0, local copies, waits for them, and re-layouts: 1.43 us -> none  [per_device(): (from_gate + from_up).reshape(n_class, per_class, n_ex, width_part)]
    unnamed x11 -> x10, local copies, waits for them, and re-layouts: 2.73 us -> 2.45 us
  transfers between devices with their start and end apart: 3 -> 3, of which waited for: 3 -> 3; matrix products, arithmetic and copies ran while one was open for 3% -> 4% of each run, Pallas kernels for 0% -> 0%
where the time goes in v5:
time: 125 us; the launch traced here: 123 us
  waiting for transfers between devices  42.2 us (34%)
  blocking collectives  34.1 us (27%)
  starting transfers between devices  26.1 us (21%)
  matrix products  9.95 us (8%)
  local copies, waits for them, and re-layouts  7.05 us (6%)
  other arithmetic  2.48 us (2%)
    all_to_all x1, blocking collectives, per_device(): got = lax.all_to_all(sent, LOCAL, 0, 0, tiled=True)  34.1 us
    all_to_all x1, waiting for transfers between devices, per_device(): back = lax.all_to_all(partial, LOCAL, 0, 0, tiled=True)  21.9 us
    all_to_all x1, starting transfers between devices, per_device(): every = lax.all_to_all(every, 'z', 0, 0, tiled=True)  15.7 us
    all_to_all x1, waiting for transfers between devices, per_device(): every = lax.all_to_all(every, 'z', 0, 0, tiled=True)  12.2 us
    all_to_all x1, waiting for transfers between devices, per_device(): lax.all_to_all(token_part.reshape(n_z, tok, width_part), 'z', 0, 0, tiled...  8.03 us
    all_to_all x1, starting transfers between devices, per_device(): back = lax.all_to_all(partial, LOCAL, 0, 0, tiled=True)  5.68 us
    all_to_all x1, starting transfers between devices, per_device(): lax.all_to_all(token_part.reshape(n_z, tok, width_part), 'z', 0, 0, tiled...  4.64 us
    dot_general x1, matrix products, per_device(): token_part = jnp.dot(picker, back, precision=lax.Precision.HIGHEST)  2.53 us
  transfers between devices with their start and end apart: 3, of which 3 were waited for; matrix products, arithmetic and copies ran while one was open for 4% of the time, Pallas kernels for 0%

profile of v5, /device:TPU:1, one launch (start us, length us, event | category | flops | bytes accessed | tf_op | source)
XLA Modules:
  0.0 122.7 jit_solution(11754181396966844539)
XLA Ops:
  0.6 0.8 convert_element_type.84
  1.6 0.7 mul.71
  2.3 0.8 copy.48
  3.3 0.8 fusion.20
  4.1 0.7 broadcast_in_dim.13
  4.8 15.7 %all-to-all-start = ((bf16[16,16,384]{2,1,0:T(8,128)(2,1)}), bf16[16,16,384]{2,1,0:T(8,128)(2,1)S(1)}, u32[]{:S(2)}, u32[]{:S(2)}) async-start(bf16[16,16,384]{2,1,0:T(8,128)(2,1)} %broadcast_in_dim.13), calls=%async_computation | async-start | bytes 393216 | tf_op jit(solution)/shard_map/all_to_all | solution.py:41
  20.9 12.2 %all-to-all-done = bf16[16,16,384]{2,1,0:T(8,128)(2,1)S(1)} async-done(((bf16[16,16,384]{2,1,0:T(8,128)(2,1)}), bf16[16,16,384]{2,1,0:T(8,128)(2,1)S(1)}, u32[]{:S(2)}, u32[]{:S(2)}) %all-to-all-start) | async-done | bytes 196640 | tf_op jit(solution)/shard_map/all_to_all | solution.py:41
  35.0 34.1 %all_to_all.20 = bf16[32,2,32,384]{3,2,1,0:T(8,128)(2,1)S(1)} all-to-all(bf16[32,2,32,384]{3,2,1,0:T(8,128)(2,1)S(1)} %bitcast.84), channel_id=1, replica_groups=mesh['z'=16,'y_lo'=2,'core'=2,'y_hi'=2,'x'=4] {'y_lo','core','y_hi','x'}, dimensions={0} | all-to-all | bytes 3145728 | tf_op jit(solution)/shard_map/all_to_all | solution.py:66
  69.7 0.4 fusion.4
  70.1 0.6 copy-done.1
  71.5 0.7 copy-done.2
  72.2 0.4 multiply_convert_fusion.1
  72.6 0.4 fusion.25
  72.9 1.5 %convolution_add_fusion = f32[4,32,8,384]{3,1,2,0:T(8,128)} fusion(f32[4,32,8,384]{3,1,2,0:T(8,128)S(1)} %fusion.25, bf16[4,32,128,1]{2,1,3,0:T(8,128)(2,1)S(1)} %bitcast.89, bf16[8,384,128,1]{2,1,0,3:T(8,128)(2,1)S(1)} %bitcast.87), kind=kOutput, calls=%fused_computation.6 | convolution fusion | flops 101056512 | bytes 3964928 | tf_op jit(solution)/shard_map/csf,edf->cesd/dot_general | solution.py:92
  74.4 5.7 %all-to-all-start.2 = ((f32[32,32,384]{2,1,0:T(8,128)}), f32[32,32,384]{2,1,0:T(8,128)}, u32[]{:S(2)}, u32[]{:S(2)}) async-start(f32[32,32,384]{2,1,0:T(8,128)} %bitcast.83), calls=%async_computation.2 | async-start | bytes 3145728 | tf_op jit(solution)/shard_map/all_to_all | solution.py:99
  80.4 21.9 %all-to-all-done.2 = f32[32,32,384]{2,1,0:T(8,128)} async-done(((f32[32,32,384]{2,1,0:T(8,128)}), f32[32,32,384]{2,1,0:T(8,128)}, u32[]{:S(2)}, u32[]{:S(2)}) %all-to-all-start.2) | async-done | bytes 1572896 | tf_op jit(solution)/shard_map/all_to_all | solution.py:99
  102.3 2.5 %fusion.10 = f32[16,4,384]{2,0,1:T(8,128)S(1)} fusion(f32[1024,384,1]{1,0,2:T(8,128)} %bitcast.24, f32[16,4,1024]{2,1,0:T(4,128)S(1)} %dot_general.35), kind=kOutput, calls=%fused_computation.18 | convolution fusion | flops 301989888 | bytes 1933312 | tf_op jit(solution)/shard_map/dot_general | solution.py:102
  104.8 0.7 copy.60
  105.5 4.6 %all-to-all-start.3 = ((f32[16,4,384]{2,1,0:T(4,128)}), f32[16,4,384]{2,1,0:T(4,128)S(1)}, u32[]{:S(2)}, u32[]{:S(2)}) async-start(f32[16,4,384]{2,1,0:T(4,128)} %copy.60), calls=%async_computation.3 | async-start | bytes 196608 | tf_op jit(solution)/shard_map/all_to_all | solution.py:103
  110.1 1.3 %fusion = bf16[1,3072,128]{2,1,0:T(8,128)(2,1)} fusion(bf16[128,3072]{1,0:T(8,128)(2,1)S(1)} %bitcast.78, bf16[128,128]{1,0:T(8,128)(2,1)S(1)} %get-tuple-element.7), kind=kOutput, calls=%fused_computation.3 | convolution fusion | flops 101056512 | bytes 1605632 | tf_op jit(solution)/shard_map/dot_general | solution.py:81
  111.4 1.3 %fusion.1 = bf16[1,3072,128]{2,1,0:T(8,128)(2,1)} fusion(bf16[128,3072]{1,0:T(8,128)(2,1)S(1)} %bitcast.79, bf16[128,128]{1,0:T(8,128)(2,1)S(1)} %get-tuple-element.6), kind=kOutput, calls=%fused_computation.4 | convolution fusion | flops 101056512 | bytes 1605632 | tf_op jit(solution)/shard_map/dot_general | solution.py:84
  112.7 1.3 %fusion.2 = bf16[1,128,3072]{2,1,0:T(8,128)(2,1)} fusion(bf16[128,3072]{1,0:T(8,128)(2,1)S(1)} %bitcast.81, f32[128,128]{1,0:T(8,128)S(1)} %fusion.6, f32[128,128]{1,0:T(8,128)S(1)} %fusion.4), kind=kOutput, calls=%fused_computation.5 | convolution fusion | flops 101154816 | bytes 1703936 | tf_op jit(solution)/shard_map/dot_general | solution.py:74
  114.0 8.0 %all-to-all-done.3 = f32[16,4,384]{2,1,0:T(4,128)S(1)} async-done(((f32[16,4,384]{2,1,0:T(4,128)}), f32[16,4,384]{2,1,0:T(4,128)S(1)}, u32[]{:S(2)}, u32[]{:S(2)}) %all-to-all-start.3) | async-done | bytes 98336 | tf_op jit(solution)/shard_map/all_to_all | solution.py:103
  122.1 0.6 reduce_sum.25
  (47 shorter events, 4.2 us)
Async XLA Ops:
  0.6 69.1 %copy-start = (bf16[1,3072,128]{2,1,0:T(8,128)(2,1)S(1)}, bf16[1,3072,128]{2,1,0:T(8,128)(2,1)}, u32[]{:S(2)}) copy-start(bf16[1,3072,128]{2,1,0:T(8,128)(2,1)} %param.11) | copy-start | bytes 2359300
  4.8 28.3 %all-to-all-start = ((bf16[16,16,384]{2,1,0:T(8,128)(2,1)}), bf16[16,16,384]{2,1,0:T(8,128)(2,1)S(1)}, u32[]{:S(2)}, u32[]{:S(2)}) async-start(bf16[16,16,384]{2,1,0:T(8,128)(2,1)} %broadcast_in_dim.13), calls=%async_computation | async-start | bytes 393216 | tf_op jit(solution)/shard_map/all_to_all | solution.py:41
  69.6 1.1 copy-start.1
  71.0 1.1 copy-start.2
  74.4 27.9 %all-to-all-start.2 = ((f32[32,32,384]{2,1,0:T(8,128)}), f32[32,32,384]{2,1,0:T(8,128)}, u32[]{:S(2)}, u32[]{:S(2)}) async-start(f32[32,32,384]{2,1,0:T(8,128)} %bitcast.83), calls=%async_computation.2 | async-start | bytes 3145728 | tf_op jit(solution)/shard_map/all_to_all | solution.py:99
  105.5 16.6 %all-to-all-start.3 = ((f32[16,4,384]{2,1,0:T(4,128)}), f32[16,4,384]{2,1,0:T(4,128)S(1)}, u32[]{:S(2)}, u32[]{:S(2)}) async-start(f32[16,4,384]{2,1,0:T(4,128)} %copy.60), calls=%async_computation.3 | async-start | bytes 196608 | tf_op jit(solution)/shard_map/all_to_all | solution.py:103

commit v6 on v5

--- a/solution.py
+++ b/solution.py
@@ -34,10 +34,8 @@
     route_row = routes.reshape(1, slots_in_block).astype(jnp.bfloat16)
     route_row = jnp.pad(route_row, ((0, 0), (0, width_part - slots_in_block)))
     pad_rows = (-(3 * tok + 1)) % 16
-    packed = jnp.concatenate(
-        [inputs, scaled, route_row, jnp.zeros((pad_rows, width_part), jnp.bfloat16)], axis=0
-    )
-    every = jnp.broadcast_to(packed[None], (n_z,) + packed.shape)
+    parts = [inputs, scaled, route_row, jnp.zeros((pad_rows, width_part), jnp.bfloat16)]
+    every = jnp.concatenate([jnp.broadcast_to(p[None], (n_z,) + p.shape) for p in parts], axis=1)
     every = lax.all_to_all(every, "z", 0, 0, tiled=True)
     class_in = every[:, :tok, :].reshape(n_z * tok, width_part)
     class_scaled = every[:, tok : 3 * tok, :].reshape(n_z * slots_in_block, width_part)
@@ -97,9 +95,9 @@
     )
     partial = (from_gate + from_up).reshape(n_class * n_ex, per_class, width_part)
     back = lax.all_to_all(partial, LOCAL, 0, 0, tiled=True)
-    back = back.reshape(n_class * n_ex * per_class, width_part)
-    picker = jnp.tile(placer_tok.astype(jnp.float32), (1, n_class))
-    token_part = jnp.dot(picker, back, precision=lax.Precision.HIGHEST)
+    back = jnp.sum(back.reshape(n_class, n_ex * per_class, width_part), axis=0)
+    token_part = jnp.take(back, column, axis=0, mode="clip")
+    token_part = jnp.sum(token_part.reshape(n_z * tok, 2, width_part), axis=1)
     owned = lax.all_to_all(token_part.reshape(n_z, tok, width_part), "z", 0, 0, tiled=True)
     input_grad = jnp.sum(owned, axis=0).astype(jnp.bfloat16)
     return (input_grad, gate_grad[None], up_grad[None], down_grad[None])

time: 125 us -> 125 us (level)
  matrix products: 9.95 us -> 7.42 us
  other arithmetic: 2.48 us -> 4.3 us
    dot_general x1 -> x0, matrix products: 2.53 us -> none  [per_device(): token_part = jnp.dot(picker, back, precision=lax.Precision.HIGHEST)]
    reduce_sum x0 -> x2, other arithmetic: none -> 1.77 us  [the longest x1 1.53 us: per_device(): back = jnp.sum(back.reshape(n_class, n_ex * per_class, width_part), axis=0)]
where the time goes in v6:
time: 125 us; the launch traced here: 123 us
  waiting for transfers between devices  42.1 us (34%)
  blocking collectives  34.1 us (27%)
  starting transfers between devices  26.1 us (21%)
  local copies, waits for them, and re-layouts  8 us (6%)
  matrix products  7.42 us (6%)
  other arithmetic  4.3 us (3%)
    all_to_all x1, blocking collectives, per_device(): got = lax.all_to_all(sent, LOCAL, 0, 0, tiled=True)  34.1 us
    all_to_all x1, waiting for transfers between devices, per_device(): back = lax.all_to_all(partial, LOCAL, 0, 0, tiled=True)  21.9 us
    all_to_all x1, starting transfers between devices, per_device(): every = lax.all_to_all(every, 'z', 0, 0, tiled=True)  15.7 us
    all_to_all x1, waiting for transfers between devices, per_device(): every = lax.all_to_all(every, 'z', 0, 0, tiled=True)  12.2 us
    all_to_all x1, waiting for transfers between devices, per_device(): lax.all_to_all(token_part.reshape(n_z, tok, width_part), 'z', 0, 0, tiled...  8.03 us
    all_to_all x1, starting transfers between devices, per_device(): back = lax.all_to_all(partial, LOCAL, 0, 0, tiled=True)  5.68 us
    all_to_all x1, starting transfers between devices, per_device(): lax.all_to_all(token_part.reshape(n_z, tok, width_part), 'z', 0, 0, tiled...  4.63 us
  transfers between devices with their start and end apart: 3, of which 3 were waited for; matrix products, arithmetic and copies ran while one was open for 4% of the time, Pallas kernels for 0%

profile of v6, /device:TPU:1, one launch (start us, length us, event | category | flops | bytes accessed | tf_op | source)
XLA Modules:
  0.0 122.9 jit_solution(10090798607971138659)
XLA Ops:
  0.6 0.8 convert_element_type.86
  1.6 0.7 mul.84
  2.3 0.8 copy.61
  3.4 0.7 broadcast_in_dim.17
  4.1 0.8 maximum_maximum_fusion
  4.9 15.7 %all-to-all-start = ((bf16[16,16,384]{2,1,0:T(8,128)(2,1)}), bf16[16,16,384]{2,1,0:T(8,128)(2,1)S(1)}, u32[]{:S(2)}, u32[]{:S(2)}) async-start(bf16[16,16,384]{2,1,0:T(8,128)(2,1)} %maximum_maximum_fusion), calls=%async_computation | async-start | bytes 393216 | tf_op jit(solution)/shard_map/all_to_all | solution.py:39
  21.0 12.2 %all-to-all-done = bf16[16,16,384]{2,1,0:T(8,128)(2,1)S(1)} async-done(((bf16[16,16,384]{2,1,0:T(8,128)(2,1)}), bf16[16,16,384]{2,1,0:T(8,128)(2,1)S(1)}, u32[]{:S(2)}, u32[]{:S(2)}) %all-to-all-start) | async-done | bytes 196640 | tf_op jit(solution)/shard_map/all_to_all | solution.py:39
  35.1 34.1 %all_to_all.20 = bf16[32,2,32,384]{3,2,1,0:T(8,128)(2,1)S(1)} all-to-all(bf16[32,2,32,384]{3,2,1,0:T(8,128)(2,1)S(1)} %bitcast.87), channel_id=1, replica_groups=mesh['z'=16,'y_lo'=2,'core'=2,'y_hi'=2,'x'=4] {'y_lo','core','y_hi','x'}, dimensions={0} | all-to-all | bytes 3145728 | tf_op jit(solution)/shard_map/all_to_all | solution.py:64
  70.2 0.6 copy-done.1
  71.6 0.7 copy-done.2
  72.3 0.4 multiply_convert_fusion.1
  72.7 0.4 fusion.19
  73.0 1.5 %convolution_add_fusion = f32[4,32,8,384]{3,1,2,0:T(8,128)} fusion(f32[4,32,8,384]{3,1,2,0:T(8,128)S(1)} %fusion.19, bf16[4,32,128,1]{2,1,3,0:T(8,128)(2,1)S(1)} %bitcast.92, bf16[8,384,128,1]{2,1,0,3:T(8,128)(2,1)S(1)} %bitcast.90), kind=kOutput, calls=%fused_computation.8 | convolution fusion | flops 101056512 | bytes 3964928 | tf_op jit(solution)/shard_map/csf,edf->cesd/dot_general | solution.py:90
  74.6 5.7 %all-to-all-start.2 = ((f32[32,32,384]{2,1,0:T(8,128)}), f32[32,32,384]{2,1,0:T(8,128)}, u32[]{:S(2)}, u32[]{:S(2)}) async-start(f32[32,32,384]{2,1,0:T(8,128)} %bitcast.86), calls=%async_computation.2 | async-start | bytes 3145728 | tf_op jit(solution)/shard_map/all_to_all | solution.py:97
  80.5 21.9 %all-to-all-done.2 = f32[32,32,384]{2,1,0:T(8,128)} async-done(((f32[32,32,384]{2,1,0:T(8,128)}), f32[32,32,384]{2,1,0:T(8,128)}, u32[]{:S(2)}, u32[]{:S(2)}) %all-to-all-start.2) | async-done | bytes 1572896 | tf_op jit(solution)/shard_map/all_to_all | solution.py:97
  102.4 1.5 %bitcast_reduce_fusion = f32[256,384]{1,0:T(8,128)S(1)} fusion(f32[4,256,384]{2,1,0:T(8,128)} %bitcast.77), kind=kLoop, calls=%fused_computation.7 | loop fusion | flops 294912 | bytes 1966080 | tf_op jit(solution)/shard_map/reduce_sum | solution.py:98
  104.0 0.8 gather_fusion
  105.1 0.7 reshape.164
  105.7 4.6 %all-to-all-start.3 = ((f32[16,4,384]{2,1,0:T(4,128)}), f32[16,4,384]{2,1,0:T(4,128)S(1)}, u32[]{:S(2)}, u32[]{:S(2)}) async-start(f32[16,4,384]{2,1,0:T(4,128)} %reshape.164), calls=%async_computation.3 | async-start | bytes 196608 | tf_op jit(solution)/shard_map/all_to_all | solution.py:101
  110.4 1.3 %fusion = bf16[1,3072,128]{2,1,0:T(8,128)(2,1)} fusion(bf16[128,3072]{1,0:T(8,128)(2,1)S(1)} %bitcast.81, bf16[128,128]{1,0:T(8,128)(2,1)S(1)} %get-tuple-element.7), kind=kOutput, calls=%fused_computation.4 | convolution fusion | flops 101056512 | bytes 1605632 | tf_op jit(solution)/shard_map/dot_general | solution.py:79
  111.7 1.3 %fusion.1 = bf16[1,3072,128]{2,1,0:T(8,128)(2,1)} fusion(bf16[128,3072]{1,0:T(8,128)(2,1)S(1)} %bitcast.82, bf16[128,128]{1,0:T(8,128)(2,1)S(1)} %get-tuple-element.6), kind=kOutput, calls=%fused_computation.5 | convolution fusion | flops 101056512 | bytes 1605632 | tf_op jit(solution)/shard_map/dot_general | solution.py:82
  113.0 1.3 %fusion.2 = bf16[1,128,3072]{2,1,0:T(8,128)(2,1)} fusion(bf16[128,3072]{1,0:T(8,128)(2,1)S(1)} %bitcast.84, f32[128,128]{1,0:T(8,128)S(1)} %fusion.6, f32[128,128]{1,0:T(8,128)S(1)} %fusion.4), kind=kOutput, calls=%fused_computation.6 | convolution fusion | flops 101154816 | bytes 1703936 | tf_op jit(solution)/shard_map/dot_general | solution.py:72
  114.3 8.0 %all-to-all-done.3 = f32[16,4,384]{2,1,0:T(4,128)S(1)} async-done(((f32[16,4,384]{2,1,0:T(4,128)}), f32[16,4,384]{2,1,0:T(4,128)S(1)}, u32[]{:S(2)}, u32[]{:S(2)}) %all-to-all-start.3) | async-done | bytes 98336 | tf_op jit(solution)/shard_map/all_to_all | solution.py:101
  122.3 0.6 reduce_sum.48
  (55 shorter events, 5.0 us)
Async XLA Ops:
  0.6 69.2 %copy-start = (bf16[1,3072,128]{2,1,0:T(8,128)(2,1)S(1)}, bf16[1,3072,128]{2,1,0:T(8,128)(2,1)}, u32[]{:S(2)}) copy-start(bf16[1,3072,128]{2,1,0:T(8,128)(2,1)} %param.11) | copy-start | bytes 2359300
  4.9 28.3 %all-to-all-start = ((bf16[16,16,384]{2,1,0:T(8,128)(2,1)}), bf16[16,16,384]{2,1,0:T(8,128)(2,1)S(1)}, u32[]{:S(2)}, u32[]{:S(2)}) async-start(bf16[16,16,384]{2,1,0:T(8,128)(2,1)} %maximum_maximum_fusion), calls=%async_computation | async-start | bytes 393216 | tf_op jit(solution)/shard_map/all_to_all | solution.py:39
  69.7 1.1 copy-start.1
  71.2 1.1 copy-start.2
  74.6 27.9 %all-to-all-start.2 = ((f32[32,32,384]{2,1,0:T(8,128)}), f32[32,32,384]{2,1,0:T(8,128)}, u32[]{:S(2)}, u32[]{:S(2)}) async-start(f32[32,32,384]{2,1,0:T(8,128)} %bitcast.86), calls=%async_computation.2 | async-start | bytes 3145728 | tf_op jit(solution)/shard_map/all_to_all | solution.py:97
  105.7 16.6 %all-to-all-start.3 = ((f32[16,4,384]{2,1,0:T(4,128)}), f32[16,4,384]{2,1,0:T(4,128)S(1)}, u32[]{:S(2)}, u32[]{:S(2)}) async-start(f32[16,4,384]{2,1,0:T(4,128)} %reshape.164), calls=%async_computation.3 | async-start | bytes 196608 | tf_op jit(solution)/shard_map/all_to_all | solution.py:101

commit v7 on v5

--- a/solution.py
+++ b/solution.py
@@ -29,9 +29,9 @@
     capacity = n_class * per_class
     slots_in_block = 2 * tok
 
-    scaled = (combine[:, :, None] * cotangent[:, None, :].astype(jnp.float32)).astype(jnp.bfloat16)
+    scaled = (combine.T[:, :, None] * cotangent[None, :, :].astype(jnp.float32)).astype(jnp.bfloat16)
     scaled = scaled.reshape(slots_in_block, width_part)
-    route_row = routes.reshape(1, slots_in_block).astype(jnp.bfloat16)
+    route_row = routes.T.reshape(1, slots_in_block).astype(jnp.bfloat16)
     route_row = jnp.pad(route_row, ((0, 0), (0, width_part - slots_in_block)))
     pad_rows = (-(3 * tok + 1)) % 16
     packed = jnp.concatenate(
@@ -49,7 +49,8 @@
     block_id = jnp.arange(n_z, dtype=jnp.int32)[:, None]
     column = (class_routes * per_class + block_id * MOST + rank).reshape(-1)
     placer = column[:, None] == jnp.arange(n_ex * per_class, dtype=jnp.int32)[None, :]
-    placer_tok = jnp.any(placer.reshape(n_z * tok, 2, n_ex * per_class), axis=1)
+    placer_tok = jnp.any(placer.reshape(n_z, 2, tok, n_ex * per_class), axis=1)
+    placer_tok = placer_tok.reshape(n_z * tok, n_ex * per_class)
 
     sent_in = jnp.dot(
         placer_tok.astype(jnp.bfloat16).T, class_in, preferred_element_type=jnp.float32

time: 125 us -> 124 us (level)
  no operation moved by 1% of the time
where the time goes in v7:
time: 124 us; the launch traced here: 122 us
  waiting for transfers between devices  42.2 us (34%)
  blocking collectives  34.1 us (28%)
  starting transfers between devices  26.1 us (21%)
  matrix products  9.95 us (8%)
  local copies, waits for them, and re-layouts  6.51 us (5%)
  other arithmetic  2.39 us (2%)
    all_to_all x1, blocking collectives, per_device(): got = lax.all_to_all(sent, LOCAL, 0, 0, tiled=True)  34.1 us
    all_to_all x1, waiting for transfers between devices, per_device(): back = lax.all_to_all(partial, LOCAL, 0, 0, tiled=True)  21.8 us
    all_to_all x1, starting transfers between devices, per_device(): every = lax.all_to_all(every, 'z', 0, 0, tiled=True)  15.7 us
    all_to_all x1, waiting for transfers between devices, per_device(): every = lax.all_to_all(every, 'z', 0, 0, tiled=True)  12.4 us
    all_to_all x1, waiting for transfers between devices, per_device(): lax.all_to_all(token_part.reshape(n_z, tok, width_part), 'z', 0, 0, tiled...  8.04 us
    all_to_all x1, starting transfers between devices, per_device(): back = lax.all_to_all(partial, LOCAL, 0, 0, tiled=True)  5.68 us
    all_to_all x1, starting transfers between devices, per_device(): lax.all_to_all(token_part.reshape(n_z, tok, width_part), 'z', 0, 0, tiled...  4.63 us
    dot_general x1, matrix products, per_device(): token_part = jnp.dot(picker, back, precision=lax.Precision.HIGHEST)  2.53 us
  transfers between devices with their start and end apart: 3, of which 3 were waited for; matrix products, arithmetic and copies ran while one was open for 4% of the time, Pallas kernels for 0%

profile of v7, /device:TPU:1, one launch (start us, length us, event | category | flops | bytes accessed | tf_op | source)
XLA Modules:
  0.0 122.1 jit_solution(8815037732467044916)
XLA Ops:
  0.6 0.8 convert_bitcast_fusion.1
  1.5 0.7 mul.71
  2.2 0.8 mul.69
  3.1 0.8 fusion.22
  3.9 0.7 broadcast_in_dim.13
  4.6 15.7 %all-to-all-start = ((bf16[16,16,384]{2,1,0:T(8,128)(2,1)}), bf16[16,16,384]{2,1,0:T(8,128)(2,1)S(1)}, u32[]{:S(2)}, u32[]{:S(2)}) async-start(bf16[16,16,384]{2,1,0:T(8,128)(2,1)} %broadcast_in_dim.13), calls=%async_computation | async-start | bytes 393216 | tf_op jit(solution)/shard_map/all_to_all | solution.py:41
  20.5 12.4 %all-to-all-done = bf16[16,16,384]{2,1,0:T(8,128)(2,1)S(1)} async-done(((bf16[16,16,384]{2,1,0:T(8,128)(2,1)}), bf16[16,16,384]{2,1,0:T(8,128)(2,1)S(1)}, u32[]{:S(2)}, u32[]{:S(2)}) %all-to-all-start) | async-done | bytes 196640 | tf_op jit(solution)/shard_map/all_to_all | solution.py:41
  34.4 34.1 %all_to_all.20 = bf16[32,2,32,384]{3,2,1,0:T(8,128)(2,1)S(1)} all-to-all(bf16[32,2,32,384]{3,2,1,0:T(8,128)(2,1)S(1)} %bitcast.90), channel_id=1, replica_groups=mesh['z'=16,'y_lo'=2,'core'=2,'y_hi'=2,'x'=4] {'y_lo','core','y_hi','x'}, dimensions={0} | all-to-all | bytes 3145728 | tf_op jit(solution)/shard_map/all_to_all | solution.py:67
  69.2 0.4 fusion.5
  69.5 0.6 copy-done.1
  70.9 0.7 copy-done.2
  71.6 0.4 multiply_convert_fusion.1
  72.0 0.4 fusion.27
  72.4 1.5 %convolution_add_fusion = f32[4,32,8,384]{3,1,2,0:T(8,128)} fusion(f32[4,32,8,384]{3,1,2,0:T(8,128)S(1)} %fusion.27, bf16[4,32,128,1]{2,1,3,0:T(8,128)(2,1)S(1)} %bitcast.94, bf16[8,384,128,1]{2,1,0,3:T(8,128)(2,1)S(1)} %bitcast.93), kind=kOutput, calls=%fused_computation.6 | convolution fusion | flops 101056512 | bytes 3964928 | tf_op jit(solution)/shard_map/csf,edf->cesd/dot_general | solution.py:93
  73.9 5.7 %all-to-all-start.2 = ((f32[32,32,384]{2,1,0:T(8,128)}), f32[32,32,384]{2,1,0:T(8,128)}, u32[]{:S(2)}, u32[]{:S(2)}) async-start(f32[32,32,384]{2,1,0:T(8,128)} %bitcast.89), calls=%async_computation.2 | async-start | bytes 3145728 | tf_op jit(solution)/shard_map/all_to_all | solution.py:100
  79.9 21.8 %all-to-all-done.2 = f32[32,32,384]{2,1,0:T(8,128)} async-done(((f32[32,32,384]{2,1,0:T(8,128)}), f32[32,32,384]{2,1,0:T(8,128)}, u32[]{:S(2)}, u32[]{:S(2)}) %all-to-all-start.2) | async-done | bytes 1572896 | tf_op jit(solution)/shard_map/all_to_all | solution.py:100
  101.8 2.5 %fusion.11 = f32[16,4,384]{2,0,1:T(8,128)S(1)} fusion(f32[1024,384,1]{1,0,2:T(8,128)} %bitcast.29, f32[16,4,1024]{2,1,0:T(4,128)S(1)} %dot_general.35), kind=kOutput, calls=%fused_computation.19 | convolution fusion | flops 301989888 | bytes 1933312 | tf_op jit(solution)/shard_map/dot_general | solution.py:103
  104.3 0.7 copy.58
  105.0 4.6 %all-to-all-start.3 = ((f32[16,4,384]{2,1,0:T(4,128)}), f32[16,4,384]{2,1,0:T(4,128)S(1)}, u32[]{:S(2)}, u32[]{:S(2)}) async-start(f32[16,4,384]{2,1,0:T(4,128)} %copy.58), calls=%async_computation.3 | async-start | bytes 196608 | tf_op jit(solution)/shard_map/all_to_all | solution.py:104
  109.6 1.3 %fusion = bf16[1,3072,128]{2,1,0:T(8,128)(2,1)} fusion(bf16[128,3072]{1,0:T(8,128)(2,1)S(1)} %bitcast.84, bf16[128,128]{1,0:T(8,128)(2,1)S(1)} %get-tuple-element.7), kind=kOutput, calls=%fused_computation.3 | convolution fusion | flops 101056512 | bytes 1605632 | tf_op jit(solution)/shard_map/dot_general | solution.py:82
  110.9 1.3 %fusion.1 = bf16[1,3072,128]{2,1,0:T(8,128)(2,1)} fusion(bf16[128,3072]{1,0:T(8,128)(2,1)S(1)} %bitcast.85, bf16[128,128]{1,0:T(8,128)(2,1)S(1)} %get-tuple-element.6), kind=kOutput, calls=%fused_computation.4 | convolution fusion | flops 101056512 | bytes 1605632 | tf_op jit(solution)/shard_map/dot_general | solution.py:85
  112.2 1.3 %fusion.2 = bf16[1,128,3072]{2,1,0:T(8,128)(2,1)} fusion(bf16[128,3072]{1,0:T(8,128)(2,1)S(1)} %bitcast.87, f32[128,128]{1,0:T(8,128)S(1)} %fusion.7, f32[128,128]{1,0:T(8,128)S(1)} %fusion.5), kind=kOutput, calls=%fused_computation.5 | convolution fusion | flops 101154816 | bytes 1703936 | tf_op jit(solution)/shard_map/dot_general | solution.py:75
  113.5 8.0 %all-to-all-done.3 = f32[16,4,384]{2,1,0:T(4,128)S(1)} async-done(((f32[16,4,384]{2,1,0:T(4,128)}), f32[16,4,384]{2,1,0:T(4,128)S(1)}, u32[]{:S(2)}, u32[]{:S(2)}) %all-to-all-start.3) | async-done | bytes 98336 | tf_op jit(solution)/shard_map/all_to_all | solution.py:104
  121.5 0.6 reduce_sum.25
  (41 shorter events, 3.6 us)
Async XLA Ops:
  0.6 68.5 %copy-start = (bf16[1,3072,128]{2,1,0:T(8,128)(2,1)S(1)}, bf16[1,3072,128]{2,1,0:T(8,128)(2,1)}, u32[]{:S(2)}) copy-start(bf16[1,3072,128]{2,1,0:T(8,128)(2,1)} %param.11) | copy-start | bytes 2359300
  4.6 28.3 %all-to-all-start = ((bf16[16,16,384]{2,1,0:T(8,128)(2,1)}), bf16[16,16,384]{2,1,0:T(8,128)(2,1)S(1)}, u32[]{:S(2)}, u32[]{:S(2)}) async-start(bf16[16,16,384]{2,1,0:T(8,128)(2,1)} %broadcast_in_dim.13), calls=%async_computation | async-start | bytes 393216 | tf_op jit(solution)/shard_map/all_to_all | solution.py:41
  69.0 1.1 copy-start.1
  70.5 1.1 copy-start.2
  73.9 27.9 %all-to-all-start.2 = ((f32[32,32,384]{2,1,0:T(8,128)}), f32[32,32,384]{2,1,0:T(8,128)}, u32[]{:S(2)}, u32[]{:S(2)}) async-start(f32[32,32,384]{2,1,0:T(8,128)} %bitcast.89), calls=%async_computation.2 | async-start | bytes 3145728 | tf_op jit(solution)/shard_map/all_to_all | solution.py:100
  105.0 16.6 %all-to-all-start.3 = ((f32[16,4,384]{2,1,0:T(4,128)}), f32[16,4,384]{2,1,0:T(4,128)S(1)}, u32[]{:S(2)}, u32[]{:S(2)}) async-start(f32[16,4,384]{2,1,0:T(4,128)} %copy.58), calls=%async_computation.3 | async-start | bytes 196608 | tf_op jit(solution)/shard_map/all_to_all | solution.py:104

commit v8 on v7

--- a/solution.py
+++ b/solution.py
@@ -1,6 +1,8 @@
 import jax
 import jax.numpy as jnp
 from jax import lax
+from jax.experimental import pallas as pl
+from jax.experimental.pallas import tpu as pltpu
 from jax.sharding import Mesh, PartitionSpec as P
 
 MOST = 2
@@ -19,6 +21,39 @@
     return (gate_pre, up_pre, gate_sig, activated, hidden)
 
 
+def pack_kernel(x_ref, cot_ref, comb_ref, rt_ref, o_ref, rows_ref):
+    tok, width = x_ref.shape
+    rows_ref[...] = jnp.zeros(rows_ref.shape, jnp.float32)
+    rows_ref[0:tok, :] = x_ref[...].astype(jnp.float32)
+    cot = cot_ref[...].astype(jnp.float32)
+    lane = lax.broadcasted_iota(jnp.int32, (1, width), 1)
+    route_row = jnp.zeros((1, width), jnp.float32)
+    for k in range(2):
+        for t in range(tok):
+            a = k * tok + t
+            row = (comb_ref[k, t] * cot[t : t + 1, :]).astype(jnp.bfloat16)
+            rows_ref[tok + a : tok + a + 1, :] = row.astype(jnp.float32)
+            route_row = jnp.where(lane == a, rt_ref[k, t].astype(jnp.float32), route_row)
+    rows_ref[3 * tok : 3 * tok + 1, :] = route_row
+    packed = rows_ref[...].astype(jnp.bfloat16)
+    for z in range(o_ref.shape[0]):
+        o_ref[z] = packed
+
+
+def pack_block(inputs, cotangent, weights, routes, copies):
+    tok, width = inputs.shape
+    rows = 3 * tok + 1 + (-(3 * tok + 1)) % 16
+    vmem = pl.BlockSpec(memory_space=pltpu.VMEM)
+    smem = pl.BlockSpec(memory_space=pltpu.SMEM)
+    return pl.pallas_call(
+        pack_kernel,
+        out_shape=jax.ShapeDtypeStruct((copies, rows, width), jnp.bfloat16),
+        in_specs=[vmem, vmem, smem, smem],
+        out_specs=vmem,
+        scratch_shapes=[pltpu.VMEM((rows, width), jnp.float32)],
+    )(inputs, cotangent, weights, routes)
+
+
 def per_device(inputs, routes, combine, cotangent, w_gate, w_up, w_down):
     tok = inputs.shape[0]
     width_part = inputs.shape[1]
@@ -29,15 +64,7 @@
     capacity = n_class * per_class
     slots_in_block = 2 * tok
 
-    scaled = (combine.T[:, :, None] * cotangent[None, :, :].astype(jnp.float32)).astype(jnp.bfloat16)
-    scaled = scaled.reshape(slots_in_block, width_part)
-    route_row = routes.T.reshape(1, slots_in_block).astype(jnp.bfloat16)
-    route_row = jnp.pad(route_row, ((0, 0), (0, width_part - slots_in_block)))
-    pad_rows = (-(3 * tok + 1)) % 16
-    packed = jnp.concatenate(
-        [inputs, scaled, route_row, jnp.zeros((pad_rows, width_part), jnp.bfloat16)], axis=0
-    )
-    every = jnp.broadcast_to(packed[None], (n_z,) + packed.shape)
+    every = pack_block(inputs, cotangent, combine.T, routes.T, n_z)
     every = lax.all_to_all(every, "z", 0, 0, tiled=True)
     class_in = every[:, :tok, :].reshape(n_z * tok, width_part)
     class_scaled = every[:, tok : 3 * tok, :].reshape(n_z * slots_in_block, width_part)

time: 124 us -> 122 us (0.984)
  local copies, waits for them, and re-layouts: 6.51 us -> 4.16 us
  Pallas kernels: 0 us -> 1.57 us
  other arithmetic: 2.39 us -> 0.86 us
    pallas_call x0 -> x1, Pallas kernels: none -> 1.57 us  [pack_block(): pl.pallas_call(pack_kernel, out_shape=jax.ShapeDtypeStruct((copies, rows,...]
    mul x3 -> x0, local copies, waits for them, and re-layouts: 1.46 us -> none  [per_device(): combine.T[:, :, None] * cotangent[None, :, :].astype(jnp.float32)]
where the time goes in v8:
time: 122 us; the launch traced here: 120 us
  waiting for transfers between devices  42.2 us (35%)
  blocking collectives  34.1 us (28%)
  starting transfers between devices  26.1 us (21%)
  matrix products  9.95 us (8%)
  local copies, waits for them, and re-layouts  4.16 us (3%)
  Pallas kernels  1.57 us (1%)
    all_to_all x1, blocking collectives, per_device(): got = lax.all_to_all(sent, LOCAL, 0, 0, tiled=True)  34.1 us
    all_to_all x1, waiting for transfers between devices, per_device(): back = lax.all_to_all(partial, LOCAL, 0, 0, tiled=True)  21.8 us
    all_to_all x1, starting transfers between devices, per_device(): every = lax.all_to_all(every, 'z', 0, 0, tiled=True)  15.7 us
    all_to_all x1, waiting for transfers between devices, per_device(): every = lax.all_to_all(every, 'z', 0, 0, tiled=True)  12.4 us
    all_to_all x1, waiting for transfers between devices, per_device(): lax.all_to_all(token_part.reshape(n_z, tok, width_part), 'z', 0, 0, tiled...  8.04 us
    all_to_all x1, starting transfers between devices, per_device(): back = lax.all_to_all(partial, LOCAL, 0, 0, tiled=True)  5.68 us
    all_to_all x1, starting transfers between devices, per_device(): lax.all_to_all(token_part.reshape(n_z, tok, width_part), 'z', 0, 0, tiled...  4.63 us
    dot_general x1, matrix products, per_device(): token_part = jnp.dot(picker, back, precision=lax.Precision.HIGHEST)  2.53 us
  transfers between devices with their start and end apart: 3, of which 3 were waited for; matrix products, arithmetic and copies ran while one was open for 4% of the time, Pallas kernels for 0%

profile of v8, /device:TPU:1, one launch (start us, length us, event | category | flops | bytes accessed | tf_op | source)
XLA Modules:
  0.0 119.8 jit_solution(2207765718404465572)
XLA Ops:
  0.6 1.6 %shard_map.102 = bf16[16,16,384]{2,1,0:T(8,128)(2,1)} custom-call(bf16[4,384]{1,0:T(4,128)(2,1)} %x_ref.1, bf16[4,384]{1,0:T(4,128)(2,1)} %cot_ref.1, f32[2,4]{1,0:T(2,128)} %bitcast.97, s32[2,4]{1,0:T(2,128)} %bitcast.98), custom_call_target="tpu_custom_call" | custom-call | tf_op jit(solution)/shard_map/pallas_call | solution.py:48
  2.2 15.7 %all-to-all-start = ((bf16[16,16,384]{2,1,0:T(8,128)(2,1)}), bf16[16,16,384]{2,1,0:T(8,128)(2,1)S(1)}, u32[]{:S(2)}, u32[]{:S(2)}) async-start(bf16[16,16,384]{2,1,0:T(8,128)(2,1)} %shard_map.102), calls=%async_computation | async-start | bytes 393216 | tf_op jit(solution)/shard_map/all_to_all | solution.py:68
  18.1 12.4 %all-to-all-done = bf16[16,16,384]{2,1,0:T(8,128)(2,1)S(1)} async-done(((bf16[16,16,384]{2,1,0:T(8,128)(2,1)}), bf16[16,16,384]{2,1,0:T(8,128)(2,1)S(1)}, u32[]{:S(2)}, u32[]{:S(2)}) %all-to-all-start) | async-done | bytes 196640 | tf_op jit(solution)/shard_map/all_to_all | solution.py:68
  31.4 0.3 convolution_convert_fusion.3
  32.1 34.1 %all_to_all.20 = bf16[32,2,32,384]{3,2,1,0:T(8,128)(2,1)S(1)} all-to-all(bf16[32,2,32,384]{3,2,1,0:T(8,128)(2,1)S(1)} %bitcast.86), channel_id=1, replica_groups=mesh['z'=16,'y_lo'=2,'core'=2,'y_hi'=2,'x'=4] {'y_lo','core','y_hi','x'}, dimensions={0} | all-to-all | bytes 3145728 | tf_op jit(solution)/shard_map/all_to_all | solution.py:94
  66.4 0.3 copy.67
  66.8 0.4 fusion.5
  67.2 0.6 copy-done.1
  67.8 0.4 fusion.7
  68.2 0.3 copy.66
  68.6 0.7 copy-done.2
  69.3 0.4 multiply_convert_fusion.1
  69.7 0.4 fusion.24
  70.1 1.5 %convolution_add_fusion = f32[4,32,8,384]{3,1,2,0:T(8,128)} fusion(f32[4,32,8,384]{3,1,2,0:T(8,128)S(1)} %fusion.24, bf16[4,32,128,1]{2,1,3,0:T(8,128)(2,1)S(1)} %bitcast.90, bf16[8,384,128,1]{2,1,0,3:T(8,128)(2,1)S(1)} %bitcast.89), kind=kOutput, calls=%fused_computation.6 | convolution fusion | flops 101056512 | bytes 3964928 | tf_op jit(solution)/shard_map/csf,edf->cesd/dot_general | solution.py:120
  71.6 5.7 %all-to-all-start.2 = ((f32[32,32,384]{2,1,0:T(8,128)}), f32[32,32,384]{2,1,0:T(8,128)}, u32[]{:S(2)}, u32[]{:S(2)}) async-start(f32[32,32,384]{2,1,0:T(8,128)} %bitcast.85), calls=%async_computation.2 | async-start | bytes 3145728 | tf_op jit(solution)/shard_map/all_to_all | solution.py:127
  77.6 21.8 %all-to-all-done.2 = f32[32,32,384]{2,1,0:T(8,128)} async-done(((f32[32,32,384]{2,1,0:T(8,128)}), f32[32,32,384]{2,1,0:T(8,128)}, u32[]{:S(2)}, u32[]{:S(2)}) %all-to-all-start.2) | async-done | bytes 1572896 | tf_op jit(solution)/shard_map/all_to_all | solution.py:127
  99.4 2.5 %fusion.11 = f32[16,4,384]{2,0,1:T(8,128)S(1)} fusion(f32[1024,384,1]{1,0,2:T(8,128)} %bitcast.29, f32[16,4,1024]{2,1,0:T(4,128)S(1)} %dot_general.35), kind=kOutput, calls=%fused_computation.19 | convolution fusion | flops 301989888 | bytes 1933312 | tf_op jit(solution)/shard_map/dot_general | solution.py:130
  102.0 0.7 copy.69
  102.6 4.6 %all-to-all-start.3 = ((f32[16,4,384]{2,1,0:T(4,128)}), f32[16,4,384]{2,1,0:T(4,128)S(1)}, u32[]{:S(2)}, u32[]{:S(2)}) async-start(f32[16,4,384]{2,1,0:T(4,128)} %copy.69), calls=%async_computation.3 | async-start | bytes 196608 | tf_op jit(solution)/shard_map/all_to_all | solution.py:131
  107.3 1.3 %fusion = bf16[1,3072,128]{2,1,0:T(8,128)(2,1)} fusion(bf16[128,3072]{1,0:T(8,128)(2,1)S(1)} %bitcast.80, bf16[128,128]{1,0:T(8,128)(2,1)S(1)} %get-tuple-element.9), kind=kOutput, calls=%fused_computation.3 | convolution fusion | flops 101056512 | bytes 1605632 | tf_op jit(solution)/shard_map/dot_general | solution.py:109
  108.6 1.3 %fusion.1 = bf16[1,3072,128]{2,1,0:T(8,128)(2,1)} fusion(bf16[128,3072]{1,0:T(8,128)(2,1)S(1)} %bitcast.81, bf16[128,128]{1,0:T(8,128)(2,1)S(1)} %get-tuple-element.8), kind=kOutput, calls=%fused_computation.4 | convolution fusion | flops 101056512 | bytes 1605632 | tf_op jit(solution)/shard_map/dot_general | solution.py:112
  109.9 1.3 %fusion.2 = bf16[1,128,3072]{2,1,0:T(8,128)(2,1)} fusion(bf16[128,3072]{1,0:T(8,128)(2,1)S(1)} %bitcast.83, f32[128,128]{1,0:T(8,128)S(1)} %fusion.7, f32[128,128]{1,0:T(8,128)S(1)} %fusion.5), kind=kOutput, calls=%fused_computation.5 | convolution fusion | flops 101154816 | bytes 1703936 | tf_op jit(solution)/shard_map/dot_general | solution.py:102
  111.2 8.0 %all-to-all-done.3 = f32[16,4,384]{2,1,0:T(4,128)S(1)} async-done(((f32[16,4,384]{2,1,0:T(4,128)}), f32[16,4,384]{2,1,0:T(4,128)S(1)}, u32[]{:S(2)}, u32[]{:S(2)}) %all-to-all-start.3) | async-done | bytes 98336 | tf_op jit(solution)/shard_map/all_to_all | solution.py:131
  119.2 0.6 reduce_sum.25
  (31 shorter events, 2.1 us)
Async XLA Ops:
  0.6 66.2 %copy-start = (bf16[1,3072,128]{2,1,0:T(8,128)(2,1)S(1)}, bf16[1,3072,128]{2,1,0:T(8,128)(2,1)}, u32[]{:S(2)}) copy-start(bf16[1,3072,128]{2,1,0:T(8,128)(2,1)} %param.11) | copy-start | bytes 2359300
  2.2 28.3 %all-to-all-start = ((bf16[16,16,384]{2,1,0:T(8,128)(2,1)}), bf16[16,16,384]{2,1,0:T(8,128)(2,1)S(1)}, u32[]{:S(2)}, u32[]{:S(2)}) async-start(bf16[16,16,384]{2,1,0:T(8,128)(2,1)} %shard_map.102), calls=%async_computation | async-start | bytes 393216 | tf_op jit(solution)/shard_map/all_to_all | solution.py:68
  66.7 1.1 copy-start.1
  68.2 1.1 copy-start.2
  71.6 27.9 %all-to-all-start.2 = ((f32[32,32,384]{2,1,0:T(8,128)}), f32[32,32,384]{2,1,0:T(8,128)}, u32[]{:S(2)}, u32[]{:S(2)}) async-start(f32[32,32,384]{2,1,0:T(8,128)} %bitcast.85), calls=%async_computation.2 | async-start | bytes 3145728 | tf_op jit(solution)/shard_map/all_to_all | solution.py:127
  102.6 16.6 %all-to-all-start.3 = ((f32[16,4,384]{2,1,0:T(4,128)}), f32[16,4,384]{2,1,0:T(4,128)S(1)}, u32[]{:S(2)}, u32[]{:S(2)}) async-start(f32[16,4,384]{2,1,0:T(4,128)} %copy.69), calls=%async_computation.3 | async-start | bytes 196608 | tf_op jit(solution)/shard_map/all_to_all | solution.py:131

commit v9 on v8

--- a/solution.py
+++ b/solution.py
@@ -52,6 +52,37 @@
         out_specs=vmem,
         scratch_shapes=[pltpu.VMEM((rows, width), jnp.float32)],
     )(inputs, cotangent, weights, routes)
+
+
+def combine_kernel(back_ref, col_ref, o_ref, sum_ref):
+    total = back_ref[0]
+    for c in range(1, back_ref.shape[0]):
+        total = total + back_ref[c]
+    sum_ref[...] = total
+    n_z, tok, width = o_ref.shape
+
+    def block(zz, carry):
+        for t in range(tok):
+            acc = jnp.zeros((1, width), jnp.float32)
+            for k in range(2):
+                col = col_ref[zz * 2 * tok + k * tok + t]
+                acc = acc + sum_ref[pl.ds(col, 1), :]
+            o_ref[zz, pl.ds(t, 1), :] = acc
+        return carry
+
+    lax.fori_loop(0, n_z, block, 0)
+
+
+def combine_tokens(back, column, n_z, tok):
+    vmem = pl.BlockSpec(memory_space=pltpu.VMEM)
+    smem = pl.BlockSpec(memory_space=pltpu.SMEM)
+    return pl.pallas_call(
+        combine_kernel,
+        out_shape=jax.ShapeDtypeStruct((n_z, tok, back.shape[2]), jnp.float32),
+        in_specs=[vmem, smem],
+        out_specs=vmem,
+        scratch_shapes=[pltpu.VMEM(back.shape[1:], jnp.float32)],
+    )(back, column)
 
 
 def per_device(inputs, routes, combine, cotangent, w_gate, w_up, w_down):
@@ -125,10 +156,9 @@
     )
     partial = (from_gate + from_up).reshape(n_class * n_ex, per_class, width_part)
     back = lax.all_to_all(partial, LOCAL, 0, 0, tiled=True)
-    back = back.reshape(n_class * n_ex * per_class, width_part)
-    picker = jnp.tile(placer_tok.astype(jnp.float32), (1, n_class))
-    token_part = jnp.dot(picker, back, precision=lax.Precision.HIGHEST)
-    owned = lax.all_to_all(token_part.reshape(n_z, tok, width_part), "z", 0, 0, tiled=True)
+    back = back.reshape(n_class, n_ex * per_class, width_part)
+    token_part = combine_tokens(back, column, n_z, tok)
+    owned = lax.all_to_all(token_part, "z", 0, 0, tiled=True)
     input_grad = jnp.sum(owned, axis=0).astype(jnp.bfloat16)
     return (input_grad, gate_grad[None], up_grad[None], down_grad[None])
 

time: 122 us -> 119 us (0.975)
  blocking collectives: 34.1 us -> 61.4 us
  waiting for transfers between devices: 42.2 us -> 20.4 us
  starting transfers between devices: 26.1 us -> 20.4 us
  matrix products: 9.95 us -> 6.26 us
  Pallas kernels: 1.57 us -> 4.03 us
    all_to_all x0 -> x1, blocking collectives: none -> 27.3 us  [per_device(): back = lax.all_to_all(partial, LOCAL, 0, 0, tiled=True)]
    all_to_all x2 -> x1, waiting for transfers between devices: 29.9 us -> 8.03 us  [per_device(): owned = lax.all_to_all(token_part, 'z', 0, 0, tiled=True)]
    all_to_all x2 -> x1, starting transfers between devices: 10.3 us -> 4.63 us  [per_device(): owned = lax.all_to_all(token_part, 'z', 0, 0, tiled=True)]
    dot_general x1 -> x0, matrix products: 2.53 us -> none  [per_device(): token_part = jnp.dot(picker, back, precision=lax.Precision.HIGHEST)]
    pallas_call x0 -> x1, Pallas kernels: none -> 2.46 us  [combine_tokens(): pl.pallas_call(combine_kernel, out_shape=jax.ShapeDtypeStruct((n_z, tok,...]
  transfers between devices with their start and end apart: 3 -> 2, of which waited for: 3 -> 2; matrix products, arithmetic and copies ran while one was open for 4% -> 3% of each run, Pallas kernels for 0% -> 0%
where the time goes in v9:
time: 119 us; the launch traced here: 117 us
  blocking collectives  61.4 us (52%)
  starting transfers between devices  20.4 us (17%)
  waiting for transfers between devices  20.4 us (17%)
  matrix products  6.26 us (5%)
  Pallas kernels  4.03 us (3%)
  local copies, waits for them, and re-layouts  3.2 us (3%)
    all_to_all x1, blocking collectives, per_device(): got = lax.all_to_all(sent, LOCAL, 0, 0, tiled=True)  34.1 us
    all_to_all x1, blocking collectives, per_device(): back = lax.all_to_all(partial, LOCAL, 0, 0, tiled=True)  27.3 us
    all_to_all x1, starting transfers between devices, per_device(): every = lax.all_to_all(every, 'z', 0, 0, tiled=True)  15.7 us
    all_to_all x1, waiting for transfers between devices, per_device(): every = lax.all_to_all(every, 'z', 0, 0, tiled=True)  12.4 us
    all_to_all x1, waiting for transfers between devices, per_device(): owned = lax.all_to_all(token_part, 'z', 0, 0, tiled=True)  8.03 us
    all_to_all x1, starting transfers between devices, per_device(): owned = lax.all_to_all(token_part, 'z', 0, 0, tiled=True)  4.63 us
    pallas_call x1, Pallas kernels, combine_tokens(): pl.pallas_call(combine_kernel, out_shape=jax.ShapeDtypeStruct((n_z, tok,...  2.46 us
  transfers between devices with their start and end apart: 2, of which 2 were waited for; matrix products, arithmetic and copies ran while one was open for 3% of the time, Pallas kernels for 0%

profile of v9, /device:TPU:1, one launch (start us, length us, event | category | flops | bytes accessed | tf_op | source)
XLA Modules:
  0.0 117.4 jit_solution(4650702482617807212)
XLA Ops:
  0.6 1.6 %shard_map.102 = bf16[16,16,384]{2,1,0:T(8,128)(2,1)} custom-call(bf16[4,384]{1,0:T(4,128)(2,1)} %x_ref.1, bf16[4,384]{1,0:T(4,128)(2,1)} %cot_ref.1, f32[2,4]{1,0:T(2,128)} %bitcast.95, s32[2,4]{1,0:T(2,128)} %bitcast.96), custom_call_target="tpu_custom_call" | custom-call | tf_op jit(solution)/shard_map/pallas_call | solution.py:48
  2.2 15.7 %all-to-all-start = ((bf16[16,16,384]{2,1,0:T(8,128)(2,1)}), bf16[16,16,384]{2,1,0:T(8,128)(2,1)S(1)}, u32[]{:S(2)}, u32[]{:S(2)}) async-start(bf16[16,16,384]{2,1,0:T(8,128)(2,1)} %shard_map.102), calls=%async_computation | async-start | bytes 393216 | tf_op jit(solution)/shard_map/all_to_all | solution.py:99
  18.1 12.4 %all-to-all-done = bf16[16,16,384]{2,1,0:T(8,128)(2,1)S(1)} async-done(((bf16[16,16,384]{2,1,0:T(8,128)(2,1)}), bf16[16,16,384]{2,1,0:T(8,128)(2,1)S(1)}, u32[]{:S(2)}, u32[]{:S(2)}) %all-to-all-start) | async-done | bytes 196640 | tf_op jit(solution)/shard_map/all_to_all | solution.py:99
  31.1 0.3 fusion.3
  31.4 0.3 convolution_convert_fusion.3
  31.9 0.2 broadcast_in_dim.8
  32.1 34.1 %all_to_all.20 = bf16[32,2,32,384]{3,2,1,0:T(8,128)(2,1)S(1)} all-to-all(bf16[32,2,32,384]{3,2,1,0:T(8,128)(2,1)S(1)} %bitcast.83), channel_id=1, replica_groups=mesh['z'=16,'y_lo'=2,'core'=2,'y_hi'=2,'x'=4] {'y_lo','core','y_hi','x'}, dimensions={0} | all-to-all | bytes 3145728 | tf_op jit(solution)/shard_map/all_to_all | solution.py:125
  66.4 0.3 copy.47
  66.9 0.4 fusion.5
  67.2 0.6 copy-done.1
  67.8 0.4 fusion.7
  68.2 0.3 copy.46
  68.6 0.7 copy-done.2
  69.3 0.4 multiply_convert_fusion.1
  69.7 0.4 fusion.22
  70.1 0.4 convolution_add_fusion
  70.5 27.3 %all_to_all.21 = f32[32,32,384]{2,1,0:T(8,128)} all-to-all(f32[32,32,384]{2,1,0:T(8,128)S(1)} %bitcast.84), channel_id=1, replica_groups=mesh['z'=16,'y_lo'=2,'core'=2,'y_hi'=2,'x'=4] {'y_lo','core','y_hi','x'}, dimensions={0} | all-to-all | bytes 3145728 | tf_op jit(solution)/shard_map/all_to_all | solution.py:158
  97.8 2.5 %shard_map.103 = f32[16,4,384]{2,1,0:T(4,128)} custom-call(f32[4,256,384]{2,1,0:T(8,128)} %bitcast.82, s32[128]{0:T(128)} %copy-done.3), custom_call_target="tpu_custom_call" | custom-call | tf_op jit(solution)/shard_map/pallas_call | solution.py:79
  100.2 4.6 %all-to-all-start.3 = ((f32[16,4,384]{2,1,0:T(4,128)}), f32[16,4,384]{2,1,0:T(4,128)S(1)}, u32[]{:S(2)}, u32[]{:S(2)}) async-start(f32[16,4,384]{2,1,0:T(4,128)} %shard_map.103), calls=%async_computation.3 | async-start | bytes 196608 | tf_op jit(solution)/shard_map/all_to_all | solution.py:161
  104.9 1.3 %fusion = bf16[1,3072,128]{2,1,0:T(8,128)(2,1)} fusion(bf16[128,3072]{1,0:T(8,128)(2,1)S(1)} %bitcast.77, bf16[128,128]{1,0:T(8,128)(2,1)S(1)} %get-tuple-element.9), kind=kOutput, calls=%fused_computation.3 | convolution fusion | flops 101056512 | bytes 1605632 | tf_op jit(solution)/shard_map/dot_general | solution.py:140
  106.2 1.3 %fusion.1 = bf16[1,3072,128]{2,1,0:T(8,128)(2,1)} fusion(bf16[128,3072]{1,0:T(8,128)(2,1)S(1)} %bitcast.78, bf16[128,128]{1,0:T(8,128)(2,1)S(1)} %get-tuple-element.8), kind=kOutput, calls=%fused_computation.4 | convolution fusion | flops 101056512 | bytes 1605632 | tf_op jit(solution)/shard_map/dot_general | solution.py:143
  107.5 1.3 %fusion.2 = bf16[1,128,3072]{2,1,0:T(8,128)(2,1)} fusion(bf16[128,3072]{1,0:T(8,128)(2,1)S(1)} %bitcast.80, f32[128,128]{1,0:T(8,128)S(1)} %fusion.7, f32[128,128]{1,0:T(8,128)S(1)} %fusion.5), kind=kOutput, calls=%fused_computation.5 | convolution fusion | flops 101154816 | bytes 1703936 | tf_op jit(solution)/shard_map/dot_general | solution.py:133
  108.7 8.0 %all-to-all-done.3 = f32[16,4,384]{2,1,0:T(4,128)S(1)} async-done(((f32[16,4,384]{2,1,0:T(4,128)}), f32[16,4,384]{2,1,0:T(4,128)S(1)}, u32[]{:S(2)}, u32[]{:S(2)}) %all-to-all-start.3) | async-done | bytes 98336 | tf_op jit(solution)/shard_map/all_to_all | solution.py:161
  116.8 0.6 reduce_sum.25
  (26 shorter events, 1.3 us)
Async XLA Ops:
  0.6 66.2 %copy-start = (bf16[1,3072,128]{2,1,0:T(8,128)(2,1)S(1)}, bf16[1,3072,128]{2,1,0:T(8,128)(2,1)}, u32[]{:S(2)}) copy-start(bf16[1,3072,128]{2,1,0:T(8,128)(2,1)} %param.11) | copy-start | bytes 2359300
  2.2 28.3 %all-to-all-start = ((bf16[16,16,384]{2,1,0:T(8,128)(2,1)}), bf16[16,16,384]{2,1,0:T(8,128)(2,1)S(1)}, u32[]{:S(2)}, u32[]{:S(2)}) async-start(bf16[16,16,384]{2,1,0:T(8,128)(2,1)} %shard_map.102), calls=%async_computation | async-start | bytes 393216 | tf_op jit(solution)/shard_map/all_to_all | solution.py:99
  31.4 0.7 copy-start.3
  66.7 1.1 copy-start.1
  68.2 1.1 copy-start.2
  100.2 16.5 %all-to-all-start.3 = ((f32[16,4,384]{2,1,0:T(4,128)}), f32[16,4,384]{2,1,0:T(4,128)S(1)}, u32[]{:S(2)}, u32[]{:S(2)}) async-start(f32[16,4,384]{2,1,0:T(4,128)} %shard_map.103), calls=%async_computation.3 | async-start | bytes 196608 | tf_op jit(solution)/shard_map/all_to_all | solution.py:161

commit v10 on v9

--- a/solution.py
+++ b/solution.py
@@ -85,6 +85,52 @@
     )(back, column)
 
 
+def row_kernel(got_ref, gw_ref, uw_ref, dw_ref, part_ref, hid_ref, gd_ref, ud_ref):
+    n_src, _, rows, width = got_ref.shape
+    n_ex = gw_ref.shape[0] // width
+    nt = (((1,), (1,)), ((), ()))
+    for c in range(n_src // n_ex):
+        gate_pre = up_pre = hidden_delta = None
+        for e in range(n_ex):
+            x_in = got_ref[c * n_ex + e, 0]
+            x_grad = got_ref[c * n_ex + e, 1]
+            span = slice(e * width, (e + 1) * width)
+            g = jnp.dot(x_in, gw_ref[span, :], preferred_element_type=jnp.float32)
+            u = jnp.dot(x_in, uw_ref[span, :], preferred_element_type=jnp.float32)
+            h = lax.dot_general(x_grad, dw_ref[:, span], nt, preferred_element_type=jnp.float32)
+            if e == 0:
+                gate_pre, up_pre, hidden_delta = g, u, h
+            else:
+                gate_pre, up_pre, hidden_delta = gate_pre + g, up_pre + u, hidden_delta + h
+        gate_sig = jax.nn.sigmoid(gate_pre)
+        activated = gate_pre * gate_sig
+        hid_ref[c * rows : (c + 1) * rows, :] = (activated * up_pre).astype(jnp.bfloat16)
+        gate_delta = (
+            hidden_delta * up_pre * gate_sig * (1.0 + gate_pre * (1.0 - gate_sig))
+        ).astype(jnp.bfloat16)
+        up_delta = (hidden_delta * activated).astype(jnp.bfloat16)
+        gd_ref[c * rows : (c + 1) * rows, :] = gate_delta
+        ud_ref[c * rows : (c + 1) * rows, :] = up_delta
+        for e in range(n_ex):
+            span = slice(e * width, (e + 1) * width)
+            part_ref[c * n_ex + e] = lax.dot_general(
+                gate_delta, gw_ref[span, :], nt, preferred_element_type=jnp.float32
+            ) + lax.dot_general(up_delta, uw_ref[span, :], nt, preferred_element_type=jnp.float32)
+
+
+def row_math(got, gate_w, up_w, down_w, n_class, n_ex):
+    n_src, _, rows, width = got.shape
+    ff = gate_w.shape[1]
+    vmem = pl.BlockSpec(memory_space=pltpu.VMEM)
+    small = jax.ShapeDtypeStruct((n_class * rows, ff), jnp.bfloat16)
+    return pl.pallas_call(
+        row_kernel,
+        out_shape=(jax.ShapeDtypeStruct((n_src, rows, width), jnp.float32), small, small, small),
+        in_specs=[vmem] * 4,
+        out_specs=(vmem, vmem, vmem, vmem),
+    )(got, gate_w, up_w, down_w)
+
+
 def per_device(inputs, routes, combine, cotangent, w_gate, w_up, w_down):
     tok = inputs.shape[0]
     width_part = inputs.shape[1]
@@ -123,38 +169,19 @@
     sent = jnp.broadcast_to(sent[None], (n_class,) + sent.shape)
     sent = sent.reshape(n_class * n_ex, 2, per_class, width_part)
     got = lax.all_to_all(sent, LOCAL, 0, 0, tiled=True)
-    got = got.reshape(n_class, n_ex, 2, per_class, width_part).transpose(2, 0, 3, 1, 4)
-    rows_in = got[0].reshape(capacity, n_ex * width_part)
-    rows_grad = got[1].reshape(capacity, n_ex * width_part)
+    rows = got.reshape(n_class, n_ex, 2, per_class, width_part).transpose(2, 0, 3, 1, 4)
+    rows_in = rows[0].reshape(capacity, n_ex * width_part)
+    rows_grad = rows[1].reshape(capacity, n_ex * width_part)
 
     gate_w, up_w, down_w = w_gate[0], w_up[0], w_down[0]
-    gate_pre, up_pre, gate_sig, activated, hidden = forward_part(rows_in, gate_w, up_w)
-    hidden_delta = jnp.dot(rows_grad, down_w.T, preferred_element_type=jnp.float32)
+    partial, hidden, gate_delta, up_delta = row_math(got, gate_w, up_w, down_w, n_class, n_ex)
     down_grad = jnp.dot(hidden.T, rows_grad, preferred_element_type=jnp.float32).astype(
         jnp.bfloat16
     )
-    gate_delta = (hidden_delta * up_pre * gate_sig * (1.0 + gate_pre * (1.0 - gate_sig))).astype(
-        jnp.bfloat16
-    )
-    up_delta = (hidden_delta * activated).astype(jnp.bfloat16)
     gate_grad = jnp.dot(rows_in.T, gate_delta, preferred_element_type=jnp.float32).astype(
         jnp.bfloat16
     )
     up_grad = jnp.dot(rows_in.T, up_delta, preferred_element_type=jnp.float32).astype(jnp.bfloat16)
-    by_slice = (n_ex, width_part, gate_w.shape[1])
-    from_gate = jnp.einsum(
-        "csf,edf->cesd",
-        gate_delta.reshape(n_class, per_class, -1),
-        gate_w.reshape(by_slice),
-        preferred_element_type=jnp.float32,
-    )
-    from_up = jnp.einsum(
-        "csf,edf->cesd",
-        up_delta.reshape(n_class, per_class, -1),
-        up_w.reshape(by_slice),
-        preferred_element_type=jnp.float32,
-    )
-    partial = (from_gate + from_up).reshape(n_class * n_ex, per_class, width_part)
     back = lax.all_to_all(partial, LOCAL, 0, 0, tiled=True)
     back = back.reshape(n_class, n_ex * per_class, width_part)
     token_part = combine_tokens(back, column, n_z, tok)

time: 119 us -> 125 us (1.050)
  blocking collectives: 61.4 us -> 34.2 us
  waiting for transfers between devices: 20.4 us -> 41.1 us
  Pallas kernels: 4.03 us -> 12.2 us
  starting transfers between devices: 20.4 us -> 25.6 us
  matrix products: 6.26 us -> 4.44 us
    all_to_all x1 -> x0, blocking collectives: 27.3 us -> none  [per_device(): back = lax.all_to_all(partial, LOCAL, 0, 0, tiled=True)]
    all_to_all x0 -> x1, waiting for transfers between devices: none -> 20.8 us  [per_device(): back = lax.all_to_all(partial, LOCAL, 0, 0, tiled=True)]
    pallas_call x0 -> x1, Pallas kernels: none -> 8.15 us  [row_math(): pl.pallas_call(row_kernel, out_shape=(jax.ShapeDtypeStruct((n_src, rows,...]
    all_to_all x0 -> x1, starting transfers between devices: none -> 5.18 us  [per_device(): back = lax.all_to_all(partial, LOCAL, 0, 0, tiled=True)]
    dot_general x5 -> x0, matrix products: 1.81 us -> none  [the longest x1 0.37 us: per_device(): jnp.dot(rows_grad, down_w.T, preferred_element_type=jnp.float32)]
  transfers between devices with their start and end apart: 2 -> 3, of which waited for: 2 -> 3; matrix products, arithmetic and copies ran while one was open for 3% -> 4% of each run, Pallas kernels for 0% -> 0%
where the time goes in v10:
time: 125 us; the launch traced here: 123 us
  waiting for transfers between devices  41.1 us (33%)
  blocking collectives  34.2 us (27%)
  starting transfers between devices  25.6 us (20%)
  Pallas kernels  12.2 us (10%)
  matrix products  4.44 us (4%)
  local copies, waits for them, and re-layouts  3.36 us (3%)
    all_to_all x1, blocking collectives, per_device(): got = lax.all_to_all(sent, LOCAL, 0, 0, tiled=True)  34.2 us
    all_to_all x1, waiting for transfers between devices, per_device(): back = lax.all_to_all(partial, LOCAL, 0, 0, tiled=True)  20.8 us
    all_to_all x1, starting transfers between devices, per_device(): every = lax.all_to_all(every, 'z', 0, 0, tiled=True)  15.7 us
    all_to_all x1, waiting for transfers between devices, per_device(): every = lax.all_to_all(every, 'z', 0, 0, tiled=True)  12.4 us
    pallas_call x1, Pallas kernels, row_math(): pl.pallas_call(row_kernel, out_shape=(jax.ShapeDtypeStruct((n_src, rows,...  8.15 us
    all_to_all x1, waiting for transfers between devices, per_device(): owned = lax.all_to_all(token_part, 'z', 0, 0, tiled=True)  7.91 us
    all_to_all x1, starting transfers between devices, per_device(): back = lax.all_to_all(partial, LOCAL, 0, 0, tiled=True)  5.18 us
    all_to_all x1, starting transfers between devices, per_device(): owned = lax.all_to_all(token_part, 'z', 0, 0, tiled=True)  4.63 us
  transfers between devices with their start and end apart: 3, of which 3 were waited for; matrix products, arithmetic and copies ran while one was open for 4% of the time, Pallas kernels for 0%

profile of v10, /device:TPU:1, one launch (start us, length us, event | category | flops | bytes accessed | tf_op | source)
XLA Modules:
  0.0 122.6 jit_solution(13775140738533607600)
XLA Ops:
  0.6 1.6 %shard_map.102 = bf16[16,16,384]{2,1,0:T(8,128)(2,1)} custom-call(bf16[4,384]{1,0:T(4,128)(2,1)} %x_ref.1, bf16[4,384]{1,0:T(4,128)(2,1)} %cot_ref.1, f32[2,4]{1,0:T(2,128)} %bitcast.59, s32[2,4]{1,0:T(2,128)} %bitcast.60), custom_call_target="tpu_custom_call" | custom-call | tf_op jit(solution)/shard_map/pallas_call | solution.py:48
  2.2 15.7 %all-to-all-start = ((bf16[16,16,384]{2,1,0:T(8,128)(2,1)}), bf16[16,16,384]{2,1,0:T(8,128)(2,1)S(1)}, u32[]{:S(2)}, u32[]{:S(2)}) async-start(bf16[16,16,384]{2,1,0:T(8,128)(2,1)} %shard_map.102), calls=%async_computation | async-start | bytes 393216 | tf_op jit(solution)/shard_map/all_to_all | solution.py:145
  18.0 0.1 add.35
  18.1 12.4 %all-to-all-done = bf16[16,16,384]{2,1,0:T(8,128)(2,1)S(1)} async-done(((bf16[16,16,384]{2,1,0:T(8,128)(2,1)}), bf16[16,16,384]{2,1,0:T(8,128)(2,1)S(1)}, u32[]{:S(2)}, u32[]{:S(2)}) %all-to-all-start) | async-done | bytes 196640 | tf_op jit(solution)/shard_map/all_to_all | solution.py:145
  30.7 0.1 reduce_sum.24
  31.1 0.3 fusion.3
  31.4 0.3 convolution_convert_fusion.3
  31.9 0.2 broadcast_in_dim.8
  32.1 34.2 %all_to_all.20.got_ref = bf16[32,2,32,384]{3,2,1,0:T(8,128)(2,1)} all-to-all(bf16[32,2,32,384]{3,2,1,0:T(8,128)(2,1)S(1)} %bitcast.47), channel_id=1, replica_groups=mesh['z'=16,'y_lo'=2,'core'=2,'y_hi'=2,'x'=4] {'y_lo','core','y_hi','x'}, dimensions={0} | all-to-all | bytes 3145728 | tf_op jit(solution)/shard_map/all_to_all | solution.py:171
  66.3 8.1 %shard_map.103 = (f32[32,32,384]{2,1,0:T(8,128)}, bf16[128,128]{1,0:T(8,128)(2,1)}, bf16[128,128]{1,0:T(8,128)(2,1)}, bf16[128,128]{1,0:T(8,128)(2,1)}) custom-call(bf16[32,2,32,384]{3,2,1,0:T(8,128)(2,1)} %all_to_all.20.got_ref, bf16[3072,128]{1,0:T(8,128)(2,1)} %bitcast.51, bf16[3072,128]{1,0:T(8,128)(2,1)} %bitcast.52, bf16[128,3072]{1,0:T(8,128)(2,1)} %bitcast.53), custom_call_target="tpu_custom_call" | custom-call | tf_op jit(solution)/shard_map/pallas_call | solution.py:126
  74.5 5.2 %all-to-all-start.2 = ((f32[32,32,384]{2,1,0:T(8,128)}), f32[32,32,384]{2,1,0:T(8,128)S(1)}, u32[]{:S(2)}, u32[]{:S(2)}) async-start(f32[32,32,384]{2,1,0:T(8,128)} %get-tuple-element.8), calls=%async_computation.2 | async-start | bytes 3145728 | tf_op jit(solution)/shard_map/all_to_all | solution.py:185
  79.6 0.9 copy.43
  80.6 0.2 fusion.11
  80.8 0.1 copy.38
  80.9 20.8 %all-to-all-done.2 = f32[32,32,384]{2,1,0:T(8,128)S(1)} async-done(((f32[32,32,384]{2,1,0:T(8,128)}), f32[32,32,384]{2,1,0:T(8,128)S(1)}, u32[]{:S(2)}, u32[]{:S(2)}) %all-to-all-start.2) | async-done | bytes 1572896 | tf_op jit(solution)/shard_map/all_to_all | solution.py:185
  101.7 1.2 copy-done.1
  102.9 2.5 %shard_map.104 = f32[16,4,384]{2,1,0:T(4,128)} custom-call(f32[4,256,384]{2,1,0:T(8,128)} %bitcast.45, s32[128]{0:T(128)} %copy-done.5), custom_call_target="tpu_custom_call" | custom-call | tf_op jit(solution)/shard_map/pallas_call | solution.py:79
  105.4 4.6 %all-to-all-start.3 = ((f32[16,4,384]{2,1,0:T(4,128)}), f32[16,4,384]{2,1,0:T(4,128)S(1)}, u32[]{:S(2)}, u32[]{:S(2)}) async-start(f32[16,4,384]{2,1,0:T(4,128)} %shard_map.104), calls=%async_computation.3 | async-start | bytes 196608 | tf_op jit(solution)/shard_map/all_to_all | solution.py:188
  110.0 1.3 %fusion = bf16[1,3072,128]{2,1,0:T(8,128)(2,1)} fusion(bf16[128,3072]{1,0:T(8,128)(2,1)S(1)} %bitcast.43, bf16[128,128]{1,0:T(8,128)(2,1)S(1)} %copy-done.4), kind=kOutput, calls=%fused_computation.3 | convolution fusion | flops 101056512 | bytes 1605632 | tf_op jit(solution)/shard_map/dot_general | solution.py:181
  111.3 0.1 copy.39
  111.5 1.3 %fusion.1 = bf16[1,3072,128]{2,1,0:T(8,128)(2,1)} fusion(bf16[128,3072]{1,0:T(8,128)(2,1)S(1)} %bitcast.44, bf16[128,128]{1,0:T(8,128)(2,1)S(1)} %copy-done.3), kind=kOutput, calls=%fused_computation.4 | convolution fusion | flops 101056512 | bytes 1605632 | tf_op jit(solution)/shard_map/dot_general | solution.py:184
  112.8 1.3 %fusion.2 = bf16[1,128,3072]{2,1,0:T(8,128)(2,1)} fusion(bf16[128,128]{1,0:T(8,128)(2,1)S(1)} %copy-done.2, bf16[128,3072]{1,0:T(8,128)(2,1)S(1)} %bitcast.48), kind=kOutput, calls=%fused_computation.5 | convolution fusion | flops 101056512 | bytes 1605632 | tf_op jit(solution)/shard_map/dot_general | solution.py:178
  114.0 7.9 %all-to-all-done.3 = f32[16,4,384]{2,1,0:T(4,128)S(1)} async-done(((f32[16,4,384]{2,1,0:T(4,128)}), f32[16,4,384]{2,1,0:T(4,128)S(1)}, u32[]{:S(2)}, u32[]{:S(2)}) %all-to-all-start.3) | async-done | bytes 98336 | tf_op jit(solution)/shard_map/all_to_all | solution.py:188
  121.9 0.6 reduce_sum.25
  (26 shorter events, 0.7 us)
Async XLA Ops:
  2.2 28.3 %all-to-all-start = ((bf16[16,16,384]{2,1,0:T(8,128)(2,1)}), bf16[16,16,384]{2,1,0:T(8,128)(2,1)S(1)}, u32[]{:S(2)}, u32[]{:S(2)}) async-start(bf16[16,16,384]{2,1,0:T(8,128)(2,1)} %shard_map.102), calls=%async_computation | async-start | bytes 393216 | tf_op jit(solution)/shard_map/all_to_all | solution.py:145
  31.4 0.7 copy-start.5
  74.5 5.2 %copy-start = (bf16[32,2,32,384]{3,2,1,0:T(8,128)(2,1)S(1)}, bf16[32,2,32,384]{3,2,1,0:T(8,128)(2,1)}, u32[]{:S(2)}) copy-start(bf16[32,2,32,384]{3,2,1,0:T(8,128)(2,1)} %all_to_all.20.got_ref) | copy-start | bytes 4718596
  74.5 27.3 %all-to-all-start.2 = ((f32[32,32,384]{2,1,0:T(8,128)}), f32[32,32,384]{2,1,0:T(8,128)S(1)}, u32[]{:S(2)}, u32[]{:S(2)}) async-start(f32[32,32,384]{2,1,0:T(8,128)} %get-tuple-element.8), calls=%async_computation.2 | async-start | bytes 3145728 | tf_op jit(solution)/shard_map/all_to_all | solution.py:185
  80.7 29.3 %copy-start.4 = (bf16[128,128]{1,0:T(8,128)(2,1)S(1)}, bf16[128,128]{1,0:T(8,128)(2,1)}, u32[]{:S(2)}) copy-start(bf16[128,128]{1,0:T(8,128)(2,1)} %get-tuple-element.9) | copy-start | bytes 98308
  101.7 1.2 copy-start.1
  105.4 16.6 %all-to-all-start.3 = ((f32[16,4,384]{2,1,0:T(4,128)}), f32[16,4,384]{2,1,0:T(4,128)S(1)}, u32[]{:S(2)}, u32[]{:S(2)}) async-start(f32[16,4,384]{2,1,0:T(4,128)} %shard_map.104), calls=%async_computation.3 | async-start | bytes 196608 | tf_op jit(solution)/shard_map/all_to_all | solution.py:188
  110.0 1.4 %copy-start.3 = (bf16[128,128]{1,0:T(8,128)(2,1)S(1)}, bf16[128,128]{1,0:T(8,128)(2,1)}, u32[]{:S(2)}) copy-start(bf16[128,128]{1,0:T(8,128)(2,1)} %get-tuple-element.10) | copy-start | bytes 98308
  111.3 1.4 %copy-start.2 = (bf16[128,128]{1,0:T(8,128)(2,1)S(1)}, bf16[128,128]{1,0:T(8,128)(2,1)}, u32[]{:S(2)}) copy-start(bf16[128,128]{1,0:T(8,128)(2,1)} %get-tuple-element.11) | copy-start | bytes 98308

commit v11 on v9

--- a/solution.py
+++ b/solution.py
@@ -70,7 +70,7 @@
             o_ref[zz, pl.ds(t, 1), :] = acc
         return carry
 
-    lax.fori_loop(0, n_z, block, 0)
+    lax.fori_loop(0, n_z, block, 0, unroll=True)
 
 
 def combine_tokens(back, column, n_z, tok):

time: 119 us -> 118 us (level)
  no operation moved by 1% of the time
where the time goes in v11:
time: 118 us; the launch traced here: 117 us
  blocking collectives  61.4 us (52%)
  starting transfers between devices  20.4 us (17%)
  waiting for transfers between devices  20.4 us (17%)
  matrix products  6.26 us (5%)
  Pallas kernels  3.88 us (3%)
  local copies, waits for them, and re-layouts  3.2 us (3%)
    all_to_all x1, blocking collectives, per_device(): got = lax.all_to_all(sent, LOCAL, 0, 0, tiled=True)  34.1 us
    all_to_all x1, blocking collectives, per_device(): back = lax.all_to_all(partial, LOCAL, 0, 0, tiled=True)  27.3 us
    all_to_all x1, starting transfers between devices, per_device(): every = lax.all_to_all(every, 'z', 0, 0, tiled=True)  15.7 us
    all_to_all x1, waiting for transfers between devices, per_device(): every = lax.all_to_all(every, 'z', 0, 0, tiled=True)  12.4 us
    all_to_all x1, waiting for transfers between devices, per_device(): owned = lax.all_to_all(token_part, 'z', 0, 0, tiled=True)  8.03 us
    all_to_all x1, starting transfers between devices, per_device(): owned = lax.all_to_all(token_part, 'z', 0, 0, tiled=True)  4.63 us
  transfers between devices with their start and end apart: 2, of which 2 were waited for; matrix products, arithmetic and copies ran while one was open for 3% of the time, Pallas kernels for 0%

profile of v11, /device:TPU:1, one launch (start us, length us, event | category | flops | bytes accessed | tf_op | source)
XLA Modules:
  0.0 117.2 jit_solution(15731798590804177040)
XLA Ops:
  0.6 1.6 %shard_map.102 = bf16[16,16,384]{2,1,0:T(8,128)(2,1)} custom-call(bf16[4,384]{1,0:T(4,128)(2,1)} %x_ref.1, bf16[4,384]{1,0:T(4,128)(2,1)} %cot_ref.1, f32[2,4]{1,0:T(2,128)} %bitcast.95, s32[2,4]{1,0:T(2,128)} %bitcast.96), custom_call_target="tpu_custom_call" | custom-call | tf_op jit(solution)/shard_map/pallas_call | solution.py:48
  2.2 15.7 %all-to-all-start = ((bf16[16,16,384]{2,1,0:T(8,128)(2,1)}), bf16[16,16,384]{2,1,0:T(8,128)(2,1)S(1)}, u32[]{:S(2)}, u32[]{:S(2)}) async-start(bf16[16,16,384]{2,1,0:T(8,128)(2,1)} %shard_map.102), calls=%async_computation | async-start | bytes 393216 | tf_op jit(solution)/shard_map/all_to_all | solution.py:99
  18.1 12.4 %all-to-all-done = bf16[16,16,384]{2,1,0:T(8,128)(2,1)S(1)} async-done(((bf16[16,16,384]{2,1,0:T(8,128)(2,1)}), bf16[16,16,384]{2,1,0:T(8,128)(2,1)S(1)}, u32[]{:S(2)}, u32[]{:S(2)}) %all-to-all-start) | async-done | bytes 196640 | tf_op jit(solution)/shard_map/all_to_all | solution.py:99
  31.1 0.3 fusion.3
  31.4 0.3 convolution_convert_fusion.3
  31.9 0.2 broadcast_in_dim.8
  32.1 34.1 %all_to_all.20 = bf16[32,2,32,384]{3,2,1,0:T(8,128)(2,1)S(1)} all-to-all(bf16[32,2,32,384]{3,2,1,0:T(8,128)(2,1)S(1)} %bitcast.83), channel_id=1, replica_groups=mesh['z'=16,'y_lo'=2,'core'=2,'y_hi'=2,'x'=4] {'y_lo','core','y_hi','x'}, dimensions={0} | all-to-all | bytes 3145728 | tf_op jit(solution)/shard_map/all_to_all | solution.py:125
  66.4 0.3 copy.47
  66.9 0.4 fusion.5
  67.2 0.6 copy-done.1
  67.8 0.4 fusion.7
  68.2 0.3 copy.46
  68.6 0.7 copy-done.2
  69.3 0.4 multiply_convert_fusion.1
  69.7 0.4 fusion.22
  70.1 0.4 convolution_add_fusion
  70.5 27.3 %all_to_all.21 = f32[32,32,384]{2,1,0:T(8,128)} all-to-all(f32[32,32,384]{2,1,0:T(8,128)S(1)} %bitcast.84), channel_id=1, replica_groups=mesh['z'=16,'y_lo'=2,'core'=2,'y_hi'=2,'x'=4] {'y_lo','core','y_hi','x'}, dimensions={0} | all-to-all | bytes 3145728 | tf_op jit(solution)/shard_map/all_to_all | solution.py:158
  97.8 2.3 %shard_map.103 = f32[16,4,384]{2,1,0:T(4,128)} custom-call(f32[4,256,384]{2,1,0:T(8,128)} %bitcast.82, s32[128]{0:T(128)} %copy-done.3), custom_call_target="tpu_custom_call" | custom-call | tf_op jit(solution)/shard_map/pallas_call | solution.py:79
  100.1 4.6 %all-to-all-start.3 = ((f32[16,4,384]{2,1,0:T(4,128)}), f32[16,4,384]{2,1,0:T(4,128)S(1)}, u32[]{:S(2)}, u32[]{:S(2)}) async-start(f32[16,4,384]{2,1,0:T(4,128)} %shard_map.103), calls=%async_computation.3 | async-start | bytes 196608 | tf_op jit(solution)/shard_map/all_to_all | solution.py:161
  104.7 1.3 %fusion = bf16[1,3072,128]{2,1,0:T(8,128)(2,1)} fusion(bf16[128,3072]{1,0:T(8,128)(2,1)S(1)} %bitcast.77, bf16[128,128]{1,0:T(8,128)(2,1)S(1)} %get-tuple-element.9), kind=kOutput, calls=%fused_computation.3 | convolution fusion | flops 101056512 | bytes 1605632 | tf_op jit(solution)/shard_map/dot_general | solution.py:140
  106.0 1.3 %fusion.1 = bf16[1,3072,128]{2,1,0:T(8,128)(2,1)} fusion(bf16[128,3072]{1,0:T(8,128)(2,1)S(1)} %bitcast.78, bf16[128,128]{1,0:T(8,128)(2,1)S(1)} %get-tuple-element.8), kind=kOutput, calls=%fused_computation.4 | convolution fusion | flops 101056512 | bytes 1605632 | tf_op jit(solution)/shard_map/dot_general | solution.py:143
  107.3 1.3 %fusion.2 = bf16[1,128,3072]{2,1,0:T(8,128)(2,1)} fusion(bf16[128,3072]{1,0:T(8,128)(2,1)S(1)} %bitcast.80, f32[128,128]{1,0:T(8,128)S(1)} %fusion.7, f32[128,128]{1,0:T(8,128)S(1)} %fusion.5), kind=kOutput, calls=%fused_computation.5 | convolution fusion | flops 101154816 | bytes 1703936 | tf_op jit(solution)/shard_map/dot_general | solution.py:133
  108.6 8.0 %all-to-all-done.3 = f32[16,4,384]{2,1,0:T(4,128)S(1)} async-done(((f32[16,4,384]{2,1,0:T(4,128)}), f32[16,4,384]{2,1,0:T(4,128)S(1)}, u32[]{:S(2)}, u32[]{:S(2)}) %all-to-all-start.3) | async-done | bytes 98336 | tf_op jit(solution)/shard_map/all_to_all | solution.py:161
  116.6 0.6 reduce_sum.25
  (26 shorter events, 1.3 us)
Async XLA Ops:
  0.6 66.2 %copy-start = (bf16[1,3072,128]{2,1,0:T(8,128)(2,1)S(1)}, bf16[1,3072,128]{2,1,0:T(8,128)(2,1)}, u32[]{:S(2)}) copy-start(bf16[1,3072,128]{2,1,0:T(8,128)(2,1)} %param.11) | copy-start | bytes 2359300
  2.2 28.3 %all-to-all-start = ((bf16[16,16,384]{2,1,0:T(8,128)(2,1)}), bf16[16,16,384]{2,1,0:T(8,128)(2,1)S(1)}, u32[]{:S(2)}, u32[]{:S(2)}) async-start(bf16[16,16,384]{2,1,0:T(8,128)(2,1)} %shard_map.102), calls=%async_computation | async-start | bytes 393216 | tf_op jit(solution)/shard_map/all_to_all | solution.py:99
  31.4 0.7 copy-start.3
  66.7 1.1 copy-start.1
  68.2 1.1 copy-start.2
  100.1 16.5 %all-to-all-start.3 = ((f32[16,4,384]{2,1,0:T(4,128)}), f32[16,4,384]{2,1,0:T(4,128)S(1)}, u32[]{:S(2)}, u32[]{:S(2)}) async-start(f32[16,4,384]{2,1,0:T(4,128)} %shard_map.103), calls=%async_computation.3 | async-start | bytes 196608 | tf_op jit(solution)/shard_map/all_to_all | solution.py:161

commit v12 on v9

--- a/solution.py
+++ b/solution.py
@@ -54,10 +54,18 @@
     )(inputs, cotangent, weights, routes)
 
 
-def combine_kernel(back_ref, col_ref, o_ref, sum_ref):
-    total = back_ref[0]
-    for c in range(1, back_ref.shape[0]):
-        total = total + back_ref[c]
+def combine_kernel(back_hbm, col_ref, o_ref, slab_ref, sum_ref, sems):
+    copies = [
+        pltpu.make_async_copy(back_hbm.at[c], slab_ref.at[c], sems.at[c])
+        for c in range(back_hbm.shape[0])
+    ]
+    for copy in copies:
+        copy.start()
+    copies[0].wait()
+    total = slab_ref[0]
+    for c in range(1, len(copies)):
+        copies[c].wait()
+        total = total + slab_ref[c]
     sum_ref[...] = total
     n_z, tok, width = o_ref.shape
 
@@ -79,9 +87,13 @@
     return pl.pallas_call(
         combine_kernel,
         out_shape=jax.ShapeDtypeStruct((n_z, tok, back.shape[2]), jnp.float32),
-        in_specs=[vmem, smem],
+        in_specs=[pl.BlockSpec(memory_space=pl.ANY), smem],
         out_specs=vmem,
-        scratch_shapes=[pltpu.VMEM(back.shape[1:], jnp.float32)],
+        scratch_shapes=[
+            pltpu.VMEM(back.shape, jnp.float32),
+            pltpu.VMEM(back.shape[1:], jnp.float32),
+            pltpu.SemaphoreType.DMA((back.shape[0],)),
+        ],
     )(back, column)
 
 

time: 119 us -> 119 us (level)
  no operation moved by 1% of the time
where the time goes in v12:
time: 119 us; the launch traced here: 118 us
  blocking collectives  61.4 us (52%)
  starting transfers between devices  20.4 us (17%)
  waiting for transfers between devices  20.4 us (17%)
  matrix products  6.26 us (5%)
  Pallas kernels  4.61 us (4%)
  local copies, waits for them, and re-layouts  3.2 us (3%)
    all_to_all x1, blocking collectives, per_device(): got = lax.all_to_all(sent, LOCAL, 0, 0, tiled=True)  34.1 us
    all_to_all x1, blocking collectives, per_device(): back = lax.all_to_all(partial, LOCAL, 0, 0, tiled=True)  27.3 us
    all_to_all x1, starting transfers between devices, per_device(): every = lax.all_to_all(every, 'z', 0, 0, tiled=True)  15.7 us
    all_to_all x1, waiting for transfers between devices, per_device(): every = lax.all_to_all(every, 'z', 0, 0, tiled=True)  12.4 us
    all_to_all x1, waiting for transfers between devices, per_device(): owned = lax.all_to_all(token_part, 'z', 0, 0, tiled=True)  8.03 us
    all_to_all x1, starting transfers between devices, per_device(): owned = lax.all_to_all(token_part, 'z', 0, 0, tiled=True)  4.65 us
    pallas_call x1, Pallas kernels, combine_tokens(): pl.pallas_call(combine_kernel, out_shape=jax.ShapeDtypeStruct((n_z, tok,...  3.05 us
  transfers between devices with their start and end apart: 2, of which 2 were waited for; matrix products, arithmetic and copies ran while one was open for 3% of the time, Pallas kernels for 0%

profile of v12, /device:TPU:1, one launch (start us, length us, event | category | flops | bytes accessed | tf_op | source)
XLA Modules:
  0.0 118.0 jit_solution(12752059980917053378)
XLA Ops:
  0.6 1.6 %shard_map.102 = bf16[16,16,384]{2,1,0:T(8,128)(2,1)} custom-call(bf16[4,384]{1,0:T(4,128)(2,1)} %x_ref.1, bf16[4,384]{1,0:T(4,128)(2,1)} %cot_ref.1, f32[2,4]{1,0:T(2,128)} %bitcast.95, s32[2,4]{1,0:T(2,128)} %bitcast.96), custom_call_target="tpu_custom_call" | custom-call | tf_op jit(solution)/shard_map/pallas_call | solution.py:48
  2.2 15.7 %all-to-all-start = ((bf16[16,16,384]{2,1,0:T(8,128)(2,1)}), bf16[16,16,384]{2,1,0:T(8,128)(2,1)S(1)}, u32[]{:S(2)}, u32[]{:S(2)}) async-start(bf16[16,16,384]{2,1,0:T(8,128)(2,1)} %shard_map.102), calls=%async_computation | async-start | bytes 393216 | tf_op jit(solution)/shard_map/all_to_all | solution.py:111
  18.1 12.4 %all-to-all-done = bf16[16,16,384]{2,1,0:T(8,128)(2,1)S(1)} async-done(((bf16[16,16,384]{2,1,0:T(8,128)(2,1)}), bf16[16,16,384]{2,1,0:T(8,128)(2,1)S(1)}, u32[]{:S(2)}, u32[]{:S(2)}) %all-to-all-start) | async-done | bytes 196640 | tf_op jit(solution)/shard_map/all_to_all | solution.py:111
  31.1 0.3 fusion.3
  31.4 0.3 convolution_convert_fusion.3
  31.9 0.2 broadcast_in_dim.8
  32.1 34.1 %all_to_all.20 = bf16[32,2,32,384]{3,2,1,0:T(8,128)(2,1)S(1)} all-to-all(bf16[32,2,32,384]{3,2,1,0:T(8,128)(2,1)S(1)} %bitcast.83), channel_id=1, replica_groups=mesh['z'=16,'y_lo'=2,'core'=2,'y_hi'=2,'x'=4] {'y_lo','core','y_hi','x'}, dimensions={0} | all-to-all | bytes 3145728 | tf_op jit(solution)/shard_map/all_to_all | solution.py:137
  66.4 0.3 copy.47
  66.9 0.4 fusion.5
  67.2 0.6 copy-done.1
  67.8 0.4 fusion.7
  68.2 0.3 copy.46
  68.6 0.7 copy-done.2
  69.3 0.4 multiply_convert_fusion.1
  69.7 0.4 fusion.22
  70.1 0.4 convolution_add_fusion
  70.5 27.3 %all_to_all.21 = f32[32,32,384]{2,1,0:T(8,128)} all-to-all(f32[32,32,384]{2,1,0:T(8,128)S(1)} %bitcast.84), channel_id=1, replica_groups=mesh['z'=16,'y_lo'=2,'core'=2,'y_hi'=2,'x'=4] {'y_lo','core','y_hi','x'}, dimensions={0} | all-to-all | bytes 3145728 | tf_op jit(solution)/shard_map/all_to_all | solution.py:170
  97.8 3.0 %shard_map.103 = f32[16,4,384]{2,1,0:T(4,128)} custom-call(f32[4,256,384]{2,1,0:T(8,128)} %bitcast.82, s32[128]{0:T(128)} %copy-done.3), custom_call_target="tpu_custom_call" | custom-call | tf_op jit(solution)/shard_map/pallas_call | solution.py:87
  100.8 4.6 %all-to-all-start.3 = ((f32[16,4,384]{2,1,0:T(4,128)}), f32[16,4,384]{2,1,0:T(4,128)S(1)}, u32[]{:S(2)}, u32[]{:S(2)}) async-start(f32[16,4,384]{2,1,0:T(4,128)} %shard_map.103), calls=%async_computation.3 | async-start | bytes 196608 | tf_op jit(solution)/shard_map/all_to_all | solution.py:173
  105.5 1.3 %fusion = bf16[1,3072,128]{2,1,0:T(8,128)(2,1)} fusion(bf16[128,3072]{1,0:T(8,128)(2,1)S(1)} %bitcast.77, bf16[128,128]{1,0:T(8,128)(2,1)S(1)} %get-tuple-element.9), kind=kOutput, calls=%fused_computation.3 | convolution fusion | flops 101056512 | bytes 1605632 | tf_op jit(solution)/shard_map/dot_general | solution.py:152
  106.8 1.3 %fusion.1 = bf16[1,3072,128]{2,1,0:T(8,128)(2,1)} fusion(bf16[128,3072]{1,0:T(8,128)(2,1)S(1)} %bitcast.78, bf16[128,128]{1,0:T(8,128)(2,1)S(1)} %get-tuple-element.8), kind=kOutput, calls=%fused_computation.4 | convolution fusion | flops 101056512 | bytes 1605632 | tf_op jit(solution)/shard_map/dot_general | solution.py:155
  108.1 1.3 %fusion.2 = bf16[1,128,3072]{2,1,0:T(8,128)(2,1)} fusion(bf16[128,3072]{1,0:T(8,128)(2,1)S(1)} %bitcast.80, f32[128,128]{1,0:T(8,128)S(1)} %fusion.7, f32[128,128]{1,0:T(8,128)S(1)} %fusion.5), kind=kOutput, calls=%fused_computation.5 | convolution fusion | flops 101154816 | bytes 1703936 | tf_op jit(solution)/shard_map/dot_general | solution.py:145
  109.4 8.0 %all-to-all-done.3 = f32[16,4,384]{2,1,0:T(4,128)S(1)} async-done(((f32[16,4,384]{2,1,0:T(4,128)}), f32[16,4,384]{2,1,0:T(4,128)S(1)}, u32[]{:S(2)}, u32[]{:S(2)}) %all-to-all-start.3) | async-done | bytes 98336 | tf_op jit(solution)/shard_map/all_to_all | solution.py:173
  117.4 0.6 reduce_sum.25
  (26 shorter events, 1.3 us)
Async XLA Ops:
  0.6 66.2 %copy-start = (bf16[1,3072,128]{2,1,0:T(8,128)(2,1)S(1)}, bf16[1,3072,128]{2,1,0:T(8,128)(2,1)}, u32[]{:S(2)}) copy-start(bf16[1,3072,128]{2,1,0:T(8,128)(2,1)} %param.11) | copy-start | bytes 2359300
  2.2 28.3 %all-to-all-start = ((bf16[16,16,384]{2,1,0:T(8,128)(2,1)}), bf16[16,16,384]{2,1,0:T(8,128)(2,1)S(1)}, u32[]{:S(2)}, u32[]{:S(2)}) async-start(bf16[16,16,384]{2,1,0:T(8,128)(2,1)} %shard_map.102), calls=%async_computation | async-start | bytes 393216 | tf_op jit(solution)/shard_map/all_to_all | solution.py:111
  31.4 0.7 copy-start.3
  66.7 1.1 copy-start.1
  68.2 1.1 copy-start.2
  100.8 16.6 %all-to-all-start.3 = ((f32[16,4,384]{2,1,0:T(4,128)}), f32[16,4,384]{2,1,0:T(4,128)S(1)}, u32[]{:S(2)}, u32[]{:S(2)}) async-start(f32[16,4,384]{2,1,0:T(4,128)} %shard_map.103), calls=%async_computation.3 | async-start | bytes 196608 | tf_op jit(solution)/shard_map/all_to_all | solution.py:173

commit v13 on v9

--- a/solution.py
+++ b/solution.py
@@ -122,14 +122,29 @@
     )
     sent = jnp.broadcast_to(sent[None], (n_class,) + sent.shape)
     sent = sent.reshape(n_class * n_ex, 2, per_class, width_part)
-    got = lax.all_to_all(sent, LOCAL, 0, 0, tiled=True)
-    got = got.reshape(n_class, n_ex, 2, per_class, width_part).transpose(2, 0, 3, 1, 4)
+    got_raw = lax.all_to_all(sent, LOCAL, 0, 0, tiled=True)
+    got = got_raw.reshape(n_class, n_ex, 2, per_class, width_part).transpose(2, 0, 3, 1, 4)
     rows_in = got[0].reshape(capacity, n_ex * width_part)
     rows_grad = got[1].reshape(capacity, n_ex * width_part)
 
     gate_w, up_w, down_w = w_gate[0], w_up[0], w_down[0]
-    gate_pre, up_pre, gate_sig, activated, hidden = forward_part(rows_in, gate_w, up_w)
-    hidden_delta = jnp.dot(rows_grad, down_w.T, preferred_element_type=jnp.float32)
+    by_slice = (n_ex, width_part, gate_w.shape[1])
+    recv = got_raw.reshape(n_class, n_ex, 2, per_class, width_part)
+    gate_pre = jnp.einsum(
+        "cesd,edf->csf", recv[:, :, 0], gate_w.reshape(by_slice), preferred_element_type=jnp.float32
+    ).reshape(capacity, -1)
+    up_pre = jnp.einsum(
+        "cesd,edf->csf", recv[:, :, 0], up_w.reshape(by_slice), preferred_element_type=jnp.float32
+    ).reshape(capacity, -1)
+    hidden_delta = jnp.einsum(
+        "cesd,fed->csf",
+        recv[:, :, 1],
+        down_w.reshape(down_w.shape[0], n_ex, width_part),
+        preferred_element_type=jnp.float32,
+    ).reshape(capacity, -1)
+    gate_sig = jax.nn.sigmoid(gate_pre)
+    activated = gate_pre * gate_sig
+    hidden = (activated * up_pre).astype(jnp.bfloat16)
     down_grad = jnp.dot(hidden.T, rows_grad, preferred_element_type=jnp.float32).astype(
         jnp.bfloat16
     )
@@ -141,7 +156,6 @@
         jnp.bfloat16
     )
     up_grad = jnp.dot(rows_in.T, up_delta, preferred_element_type=jnp.float32).astype(jnp.bfloat16)
-    by_slice = (n_ex, width_part, gate_w.shape[1])
     from_gate = jnp.einsum(
         "csf,edf->cesd",
         gate_delta.reshape(n_class, per_class, -1),

time: 119 us -> 122 us (1.025)
  blocking collectives: 61.4 us -> 0 us
  waiting for transfers between devices: 20.4 us -> 62.7 us
  starting transfers between devices: 20.4 us -> 38.9 us
  local copies, waits for them, and re-layouts: 3.2 us -> 5.05 us
    all_to_all x2 -> x0, blocking collectives: 61.4 us -> none  [the longest x1 34.1 us: per_device(): got = lax.all_to_all(sent, LOCAL, 0, 0, tiled=True)]
    all_to_all x0 -> x2, waiting for transfers between devices: none -> 42.6 us  [the longest x1 21.6 us: per_device(): back = lax.all_to_all(partial, LOCAL, 0, 0, tiled=True)]
    all_to_all x0 -> x2, starting transfers between devices: none -> 18.5 us  [the longest x1 12.1 us: per_device(): got_raw = lax.all_to_all(sent, LOCAL, 0, 0, tiled=True)]
  transfers between devices with their start and end apart: 2 -> 4, of which waited for: 2 -> 4; matrix products, arithmetic and copies ran while one was open for 3% -> 5% of each run, Pallas kernels for 0% -> 0%
where the time goes in v13:
time: 122 us; the launch traced here: 120 us
  waiting for transfers between devices  62.7 us (51%)
  starting transfers between devices  38.9 us (32%)
  matrix products  7.47 us (6%)
  local copies, waits for them, and re-layouts  5.05 us (4%)
  Pallas kernels  4.04 us (3%)
    all_to_all x1, waiting for transfers between devices, per_device(): back = lax.all_to_all(partial, LOCAL, 0, 0, tiled=True)  21.6 us
    all_to_all x1, waiting for transfers between devices, per_device(): got_raw = lax.all_to_all(sent, LOCAL, 0, 0, tiled=True)  21.1 us
    all_to_all x1, starting transfers between devices, per_device(): every = lax.all_to_all(every, 'z', 0, 0, tiled=True)  15.7 us
    all_to_all x1, waiting for transfers between devices, per_device(): every = lax.all_to_all(every, 'z', 0, 0, tiled=True)  12.4 us
    all_to_all x1, starting transfers between devices, per_device(): got_raw = lax.all_to_all(sent, LOCAL, 0, 0, tiled=True)  12.1 us
    all_to_all x1, waiting for transfers between devices, per_device(): owned = lax.all_to_all(token_part, 'z', 0, 0, tiled=True)  7.65 us
    all_to_all x1, starting transfers between devices, per_device(): back = lax.all_to_all(partial, LOCAL, 0, 0, tiled=True)  6.44 us
    all_to_all x1, starting transfers between devices, per_device(): owned = lax.all_to_all(token_part, 'z', 0, 0, tiled=True)  4.63 us
  transfers between devices with their start and end apart: 4, of which 4 were waited for; matrix products, arithmetic and copies ran while one was open for 5% of the time, Pallas kernels for 0%

profile of v13, /device:TPU:1, one launch (start us, length us, event | category | flops | bytes accessed | tf_op | source)
XLA Modules:
  0.0 119.8 jit_solution(3067009183738709480)
XLA Ops:
  0.6 1.6 %shard_map.102 = bf16[16,16,384]{2,1,0:T(8,128)(2,1)} custom-call(bf16[4,384]{1,0:T(4,128)(2,1)} %x_ref.1, bf16[4,384]{1,0:T(4,128)(2,1)} %cot_ref.1, f32[2,4]{1,0:T(2,128)} %bitcast.109, s32[2,4]{1,0:T(2,128)} %bitcast.110), custom_call_target="tpu_custom_call" | custom-call | tf_op jit(solution)/shard_map/pallas_call | solution.py:48
  2.2 15.7 %all-to-all-start = ((bf16[16,16,384]{2,1,0:T(8,128)(2,1)}), bf16[16,16,384]{2,1,0:T(8,128)(2,1)S(1)}, u32[]{:S(2)}, u32[]{:S(2)}) async-start(bf16[16,16,384]{2,1,0:T(8,128)(2,1)} %shard_map.102), calls=%async_computation | async-start | bytes 393216 | tf_op jit(solution)/shard_map/all_to_all | solution.py:99
  18.1 12.4 %all-to-all-done = bf16[16,16,384]{2,1,0:T(8,128)(2,1)S(1)} async-done(((bf16[16,16,384]{2,1,0:T(8,128)(2,1)}), bf16[16,16,384]{2,1,0:T(8,128)(2,1)S(1)}, u32[]{:S(2)}, u32[]{:S(2)}) %all-to-all-start) | async-done | bytes 196640 | tf_op jit(solution)/shard_map/all_to_all | solution.py:99
  31.4 0.3 convolution_convert_fusion.3
  31.9 1.4 %broadcast_in_dim.8 = bf16[4,8,2,32,384]{4,3,2,1,0:T(8,128)(2,1)} broadcast(bf16[8,2,32,384]{3,2,1,0:T(8,128)(2,1)S(1)} %copy.45), dimensions={1,2,3,4} | broadcast | bytes 1966080 | tf_op jit(solution)/shard_map/broadcast_in_dim | solution.py:123
  33.3 12.1 %all-to-all-start.1 = ((bf16[32,2,32,384]{3,2,1,0:T(8,128)(2,1)}), bf16[32,2,32,384]{3,2,1,0:T(8,128)(2,1)S(1)}, u32[]{:S(2)}, u32[]{:S(2)}) async-start(bf16[32,2,32,384]{3,2,1,0:T(8,128)(2,1)} %bitcast.93), calls=%async_computation.1 | async-start | bytes 3145728 | tf_op jit(solution)/shard_map/all_to_all | solution.py:125
  45.4 1.0 copy.53
  46.4 21.1 %all-to-all-done.1 = bf16[32,2,32,384]{3,2,1,0:T(8,128)(2,1)S(1)} async-done(((bf16[32,2,32,384]{3,2,1,0:T(8,128)(2,1)}), bf16[32,2,32,384]{3,2,1,0:T(8,128)(2,1)S(1)}, u32[]{:S(2)}, u32[]{:S(2)}) %all-to-all-start.1) | async-done | bytes 1572896 | tf_op jit(solution)/shard_map/all_to_all | solution.py:125
  67.9 0.4 convolution_bitcast_fusion.1
  68.3 0.6 copy-done.1
  68.9 0.4 convolution_bitcast_fusion.2
  69.3 0.4 multiply_convert_fusion.1
  69.7 0.4 fusion.17
  70.0 1.5 %convolution_add_fusion = f32[4,32,8,384]{3,1,2,0:T(8,128)} fusion(f32[4,32,8,384]{3,1,2,0:T(8,128)S(1)} %fusion.17, bf16[4,32,128,1]{2,1,3,0:T(8,128)(2,1)S(1)} %bitcast.105, bf16[8,384,128,1]{2,1,0,3:T(8,128)(2,1)S(1)} %bitcast.98), kind=kOutput, calls=%fused_computation.6 | convolution fusion | flops 101056512 | bytes 3964928 | tf_op jit(solution)/shard_map/csf,edf->cesd/dot_general | solution.py:165
  71.6 6.4 %all-to-all-start.2 = ((f32[32,32,384]{2,1,0:T(8,128)}), f32[32,32,384]{2,1,0:T(8,128)}, u32[]{:S(2)}, u32[]{:S(2)}) async-start(f32[32,32,384]{2,1,0:T(8,128)} %bitcast.92), calls=%async_computation.2 | async-start | bytes 3145728 | tf_op jit(solution)/shard_map/all_to_all | solution.py:172
  78.2 0.3 copy.49
  78.6 21.6 %all-to-all-done.2 = f32[32,32,384]{2,1,0:T(8,128)} async-done(((f32[32,32,384]{2,1,0:T(8,128)}), f32[32,32,384]{2,1,0:T(8,128)}, u32[]{:S(2)}, u32[]{:S(2)}) %all-to-all-start.2) | async-done | bytes 1572896 | tf_op jit(solution)/shard_map/all_to_all | solution.py:172
  100.2 2.5 %shard_map.103 = f32[16,4,384]{2,1,0:T(4,128)} custom-call(f32[4,256,384]{2,1,0:T(8,128)} %bitcast.32.back_ref, s32[128]{0:T(128)} %copy-done.4), custom_call_target="tpu_custom_call" | custom-call | tf_op jit(solution)/shard_map/pallas_call | solution.py:79
  102.6 4.6 %all-to-all-start.3 = ((f32[16,4,384]{2,1,0:T(4,128)}), f32[16,4,384]{2,1,0:T(4,128)S(1)}, u32[]{:S(2)}, u32[]{:S(2)}) async-start(f32[16,4,384]{2,1,0:T(4,128)} %shard_map.103), calls=%async_computation.3 | async-start | bytes 196608 | tf_op jit(solution)/shard_map/all_to_all | solution.py:175
  107.3 1.3 %fusion.1 = bf16[1,3072,128]{2,1,0:T(8,128)(2,1)} fusion(bf16[128,3072]{1,0:T(8,128)(2,1)S(1)} %bitcast.88, bf16[128,128]{1,0:T(8,128)(2,1)S(1)} %get-tuple-element.10), kind=kOutput, calls=%fused_computation.4 | convolution fusion | flops 101056512 | bytes 1605632 | tf_op jit(solution)/shard_map/dot_general | solution.py:158
  109.0 1.3 %fusion = bf16[1,3072,128]{2,1,0:T(8,128)(2,1)} fusion(bf16[128,3072]{1,0:T(8,128)(2,1)S(1)} %bitcast.89, bf16[128,128]{1,0:T(8,128)(2,1)S(1)} %get-tuple-element.11), kind=kOutput, calls=%fused_computation.3 | convolution fusion | flops 101056512 | bytes 1605632 | tf_op jit(solution)/shard_map/dot_general | solution.py:155
  110.3 1.3 %fusion.2 = bf16[1,128,3072]{2,1,0:T(8,128)(2,1)} fusion(bf16[128,3072]{1,0:T(8,128)(2,1)S(1)} %bitcast.96, f32[128,128]{1,0:T(8,128)S(1)} %convolution_bitcast_fusion.2, f32[128,128]{1,0:T(8,128)S(1)} %convolution_bitcast_fusion.1), kind=kOutput, calls=%fused_computation.5 | convolution fusion | flops 101154816 | bytes 1703936 | tf_op jit(solution)/shard_map/dot_general | solution.py:148
  111.6 7.6 %all-to-all-done.3 = f32[16,4,384]{2,1,0:T(4,128)S(1)} async-done(((f32[16,4,384]{2,1,0:T(4,128)}), f32[16,4,384]{2,1,0:T(4,128)S(1)}, u32[]{:S(2)}, u32[]{:S(2)}) %all-to-all-start.3) | async-done | bytes 98336 | tf_op jit(solution)/shard_map/all_to_all | solution.py:175
  119.2 0.6 reduce_sum.25
  (34 shorter events, 2.2 us)
Async XLA Ops:
  0.6 67.2 %copy-start = (bf16[1,3072,128]{2,1,0:T(8,128)(2,1)S(1)}, bf16[1,3072,128]{2,1,0:T(8,128)(2,1)}, u32[]{:S(2)}) copy-start(bf16[1,3072,128]{2,1,0:T(8,128)(2,1)} %param.11) | copy-start | bytes 2359300
  2.2 28.3 %all-to-all-start = ((bf16[16,16,384]{2,1,0:T(8,128)(2,1)}), bf16[16,16,384]{2,1,0:T(8,128)(2,1)S(1)}, u32[]{:S(2)}, u32[]{:S(2)}) async-start(bf16[16,16,384]{2,1,0:T(8,128)(2,1)} %shard_map.102), calls=%async_computation | async-start | bytes 393216 | tf_op jit(solution)/shard_map/all_to_all | solution.py:99
  31.4 1.9 %copy-start.4 = (s32[128]{0:T(128)}, s32[128]{0:T(128)S(1)}, u32[]{:S(2)}) copy-start(s32[128]{0:T(128)S(1)} %add_add_fusion.1.col_ref) | copy-start | bytes 1540
  33.3 12.1 %copy-start.2 = (bf16[1,128,3072]{2,1,0:T(8,128)(2,1)S(1)}, bf16[1,128,3072]{2,1,0:T(8,128)(2,1)}, u32[]{:S(2)}) copy-start(bf16[1,128,3072]{2,1,0:T(8,128)(2,1)} %param.13) | copy-start | bytes 2359300
  33.3 34.2 %all-to-all-start.1 = ((bf16[32,2,32,384]{3,2,1,0:T(8,128)(2,1)}), bf16[32,2,32,384]{3,2,1,0:T(8,128)(2,1)S(1)}, u32[]{:S(2)}, u32[]{:S(2)}) async-start(bf16[32,2,32,384]{3,2,1,0:T(8,128)(2,1)} %bitcast.93), calls=%async_computation.1 | async-start | bytes 3145728 | tf_op jit(solution)/shard_map/all_to_all | solution.py:125
  67.8 1.1 copy-start.1
  67.9 1.4 %copy-start.3 = (bf16[16,8,8,384]{3,2,1,0:T(8,128)(2,1)S(1)}, bf16[16,8,8,384]{3,2,1,0:T(8,128)(2,1)}, u32[]{:S(2)}) copy-start(bf16[16,8,8,384]{3,2,1,0:T(8,128)(2,1)} %copy.53) | copy-start | bytes 2359300
  71.6 28.6 %all-to-all-start.2 = ((f32[32,32,384]{2,1,0:T(8,128)}), f32[32,32,384]{2,1,0:T(8,128)}, u32[]{:S(2)}, u32[]{:S(2)}) async-start(f32[32,32,384]{2,1,0:T(8,128)} %bitcast.92), calls=%async_computation.2 | async-start | bytes 3145728 | tf_op jit(solution)/shard_map/all_to_all | solution.py:172
  102.6 16.6 %all-to-all-start.3 = ((f32[16,4,384]{2,1,0:T(4,128)}), f32[16,4,384]{2,1,0:T(4,128)S(1)}, u32[]{:S(2)}, u32[]{:S(2)}) async-start(f32[16,4,384]{2,1,0:T(4,128)} %shard_map.103), calls=%async_computation.3 | async-start | bytes 196608 | tf_op jit(solution)/shard_map/all_to_all | solution.py:175
